TPU v7x, 256 devices: a whole 4x4x8 slice. The times are simulated.
256 devices in a mesh: docs: 32 (over y, x, z_hi), dims: 8 (over z_lo, core).
Axes of the slice: x: 4, y: 4, z: 8 (z_hi: 2, z_lo: 4; z = z_hi * 4 + z_lo), core: 2. Of those that a mesh axis runs over, the one named last changes fastest.
Arguments:
- queries: bfloat16 [16384, 3072], P('docs', 'dims'), may hold values from -6 to 6
- doc_vectors: bfloat16 [65536, 3072], P('docs', 'dims'), may hold values from -6 to 6
- surv_pairs: int32 [32, 144], P('docs'), may hold values from 0 to 2047
- surv_count: int32 [32], P('docs'), may hold values from 36 to 144, as said below
- short_pairs: int32 [32, 96], P('docs'), may hold values from 0 to 2047
- short_count: int32 [32], P('docs'), may hold values from 24 to 96, as said below
Outputs:
- prefix_scores: float32 [32, 144, 128, 128], P('docs', None, 'dims')
- full_scores: float32 [32, 96, 128, 128], P('docs', None, 'dims')
Inputs may be any that keep to these rules, and one draw needn't show every extreme that they name: `surv_count`: each shard's live survivor slots; some shard has all 144 slots live. `short_count`: each shard's live shortlist slots; some shard has all 96 slots live.
All inputs are finite; a program needn't handle non-finite values.
Results may differ from a plain program's by a relative error of at most 0.0003.
Values may be sent and summed in bfloat16 or wider, within the bound.
No kernel may reach another device: no remote copies, remote signals or barrier semaphores. Data moves between devices by JAX's collectives and lax.ppermute only.
A program may use at most 128 MiB of HBM per device.

v0:
```python
import jax
import jax.numpy as jnp
from jax import lax
from jax.sharding import PartitionSpec as P

D = 3072
PREFIX = 768
QB = 128
DB = 128


def shards(queries, doc_vectors, surv_pairs, surv_count, short_pairs, short_count):
    every_query = lax.all_gather(queries, "docs", axis=0, tiled=True)
    slice_width = queries.shape[1]
    query_blocks = every_query.reshape(-1, QB, slice_width)
    doc_blocks = doc_vectors.reshape(-1, DB, slice_width)
    local_blocks = doc_blocks.shape[0]
    columns = lax.axis_index("dims") * slice_width + jnp.arange(slice_width)
    prefix_blocks = jnp.where(
        columns[None, None, :] < PREFIX, doc_blocks, jnp.zeros((), doc_blocks.dtype)
    )

    def pair_products(pair_ids, doc_side):
        picked_queries = jnp.take(query_blocks, pair_ids // local_blocks, axis=0)
        picked_docs = jnp.take(doc_side, pair_ids % local_blocks, axis=0)
        return jnp.einsum(
            "gqc,gdc->gqd", picked_queries, picked_docs, preferred_element_type=jnp.float32
        )

    def score_slots(pair_list, doc_side):
        return pair_products(pair_list, doc_side)

    full_terms = score_slots(short_pairs[0], doc_blocks)
    prefix_terms = score_slots(surv_pairs[0], prefix_blocks)
    prefix_sum, full_sum = (
        lax.psum_scatter(prefix_terms, "dims", scatter_dimension=1, tiled=True),
        lax.psum_scatter(full_terms, "dims", scatter_dimension=1, tiled=True),
    )

    def finish(summed, live_count, factor):
        slots = jnp.arange(summed.shape[0])
        return jnp.where(slots[:, None, None] < live_count, summed * factor, jnp.float32(0.0))

    prefix_out = finish(prefix_sum, surv_count[0], float(PREFIX) ** (-0.5))
    full_out = finish(full_sum, short_count[0], float(D) ** (-0.5))
    return (prefix_out[None], full_out[None])


def solution(mesh):
    placed = (
        P("docs", "dims"),
        P("docs", "dims"),
        P("docs", None),
        P("docs"),
        P("docs", None),
        P("docs"),
    )
    return jax.shard_map(
        shards,
        mesh=mesh,
        in_specs=placed,
        out_specs=(P("docs", None, "dims", None), P("docs", None, "dims", None)),
        check_vma=False,
    )
```

profile of v0, /device:TPU:2, one launch (start us, length us, event | category | flops | bytes accessed | tf_op | source)
XLA Modules:
  0.0 420.8 jit_solution(5105553798239716115)
XLA Ops:
  7.2 0.0 all-gather.2.cloned.1.call-start
  7.2 0.7 all-gather.2.cloned.1.call-update
  7.9 0.0 reduce-scatter.5.cloned.1.call-start
  7.9 0.7 fusion.12
  8.6 0.0 copy-start.2
  8.6 9.3 %gather_fusion.3 = bf16[96,128,384]{2,1,0:T(8,128)(2,1)} fusion(bf16[16,128,384]{2,1,0:T(8,128)(2,1)} %bitcast.65, s32[1024]{0:T(1024)S(1)} %get-tuple-element.10), kind=kCustom, calls=%fused_computation.3 | custom fusion | bytes 18874752 | tf_op jit(solution)/shard_map/jit(_take)/gather | solution.py:25
  17.9 0.0 copy-done.2
  17.9 195.3 %all-gather.2.cloned.1.call-done = bf16[16384,384]{1,0:T(8,128)(2,1)} async-done(((bf16[512,384]{1,0:T(8,128)(2,1)}), bf16[16384,384]{1,0:T(8,128)(2,1)}) %all-gather.2.cloned.1.call-update) | async-done | bytes 12582928 | tf_op jit(solution)/shard_map/all_gather | solution.py:13
  213.2 12.5 %gather_fusion.2 = bf16[96,128,384]{2,1,0:T(8,128)(2,1)} fusion(bf16[128,128,384]{2,1,0:T(8,128)(2,1)} %bitcast.67, s32[1024]{0:T(1024)S(1)} %get-tuple-element.11), kind=kCustom, calls=%fused_computation.2 | custom fusion | bytes 18874752 | tf_op jit(solution)/shard_map/jit(_take)/gather | solution.py:24
  225.7 0.0 copy-start.1
  225.7 0.0 copy-start
  225.7 10.4 %fusion.5 = f32[96,128,128]{2,1,0:T(8,128)} fusion(bf16[96,128,384]{2,1,0:T(8,128)(2,1)} %gather_fusion.3, bf16[96,128,384]{2,1,0:T(8,128)(2,1)} %gather_fusion.2, pred[96]{0:T(512)(128)(4,1)S(1)} %get-tuple-element.7, pred[96]{0:T(512)(128)(4,1)S(1)} %get-tuple-element.6), kind=kOutput, calls=%fused_computation.9 | convolution fusion | flops 1217396736 | bytes 25166016 | tf_op jit(solution)/shard_map/gqc,gdc->gqd/dot_general | solution.py:26
  236.1 0.0 reduce-scatter.5.cloned.1.call-update
  236.1 0.2 reduce-scatter.3.cloned.1.call-start
  236.4 0.0 copy-done.1
  236.4 0.0 copy-done
  236.5 0.2 broadcast_select_fusion
  236.6 9.5 %gather_fusion.1 = bf16[144,128,384]{2,1,0:T(8,128)(2,1)} fusion(bf16[16,128,384]{2,1,0:T(8,128)(2,1)S(1)} %broadcast_select_fusion, s32[1024]{0:T(1024)S(1)} %pad_clamp_fusion.2), kind=kCustom, calls=%fused_computation.1 | custom fusion | bytes 28312128 | tf_op jit(solution)/shard_map/jit(_take)/gather | solution.py:25
  246.1 14.2 %gather_fusion = bf16[144,128,384]{2,1,0:T(8,128)(2,1)} fusion(bf16[128,128,384]{2,1,0:T(8,128)(2,1)} %bitcast.68, s32[1024]{0:T(1024)S(1)} %pad_clamp_fusion.3), kind=kCustom, calls=%fused_computation | custom fusion | bytes 28312128 | tf_op jit(solution)/shard_map/jit(_take)/gather | solution.py:24
  260.3 14.8 %fusion = f32[144,128,128]{2,1,0:T(8,128)} fusion(bf16[144,128,384]{2,1,0:T(8,128)(2,1)} %gather_fusion.1, bf16[144,128,384]{2,1,0:T(8,128)(2,1)} %gather_fusion, pred[144]{0:T(512)(128)(4,1)S(1)} %get-tuple-element.5, pred[144]{0:T(512)(128)(4,1)S(1)} %get-tuple-element.4), kind=kOutput, calls=%fused_computation.4 | convolution fusion | flops 1826095104 | bytes 37749024 | tf_op jit(solution)/shard_map/gqc,gdc->gqd/dot_general | solution.py:26
  275.2 0.0 reduce-scatter.3.cloned.1.call-update
  276.5 29.4 %reduce-scatter.5.cloned.1.call-done = f32[96,16,128]{2,1,0:T(8,128)} async-done(((f32[96,128,128]{2,1,0:T(8,128)}), f32[96,16,128]{2,1,0:T(8,128)}) %reduce-scatter.5.cloned.1.call-update) | async-done | bytes 786448 | tf_op jit(solution)/shard_map/reduce_scatter | solution.py:37
  305.9 2.2 select_bitcast_fusion.1
  308.1 103.7 %reduce-scatter.3.cloned.1.call-done = f32[144,16,128]{2,1,0:T(8,128)} async-done(((f32[144,128,128]{2,1,0:T(8,128)}), f32[144,16,128]{2,1,0:T(8,128)}) %reduce-scatter.3.cloned.1.call-update) | async-done | bytes 1179664 | tf_op jit(solution)/shard_map/reduce_scatter | solution.py:36
  411.8 2.5 select_bitcast_fusion
  (10 shorter events, 0.1 us)
Async XLA Ops:
  7.2 206.0 %all-gather.2.cloned.1.call-start = ((), (), s32[]{:S(2)}) async-start(), calls=%async_computation.2 | async-start | bytes 12976128 | tf_op jit(solution)/shard_map/all_gather | solution.py:13
  7.9 298.0 %reduce-scatter.5.cloned.1.call-start = ((), (), s32[]{:S(2)}) async-start(), calls=%async_computation.4 | async-start | bytes 7077888 | tf_op jit(solution)/shard_map/reduce_scatter | solution.py:37
  8.6 9.3 %copy-start.2 = (s32[1,96]{1,0:T(1,128)S(1)}, s32[1,96]{1,0:T(1,128)}, u32[]{:S(2)}) copy-start(s32[1,96]{1,0:T(1,128)} %param.10) | copy-start | bytes 1156
  225.7 10.7 %copy-start.1 = (s32[1,144]{1,0:T(1,128)S(1)}, s32[1,144]{1,0:T(1,128)}, u32[]{:S(2)}) copy-start(s32[1,144]{1,0:T(1,128)} %param.8) | copy-start | bytes 1732
  225.7 10.8 %copy-start = (bf16[2048,384]{1,0:T(8,128)(2,1)S(1)}, bf16[2048,384]{1,0:T(8,128)(2,1)}, u32[]{:S(2)}) copy-start(bf16[2048,384]{1,0:T(8,128)(2,1)} %param.7) | copy-start | bytes 4718596
  236.1 175.6 %reduce-scatter.3.cloned.1.call-start = ((), (), s32[]{:S(2)}) async-start(), calls=%async_computation.3 | async-start | bytes 10616832 | tf_op jit(solution)/shard_map/reduce_scatter | solution.py:36
Sparse Core Ops, SparseCore 0:
  11.5 201.6 all-gather.1
  236.3 69.5 reduce-scatter.4
  308.4 103.2 reduce-scatter.2
where the time goes:
time: 421 us
  waiting for transfers between devices  329 us (78%)
  local copies, waits for them, and re-layouts  45.5 us (11%)
  matrix products  25.3 us (6%)
  between operations  15.1 us (4%)
  other arithmetic  5.6 us (1%)
    all_gather x1, waiting for transfers between devices, shards(): every_query = lax.all_gather(queries, 'docs', axis=0, tiled=True)  195 us
    reduce_scatter x1, waiting for transfers between devices, shards(): lax.psum_scatter(prefix_terms, 'dims', scatter_dimension=1, tiled=True)  104 us
    reduce_scatter x1, waiting for transfers between devices, shards(): lax.psum_scatter(full_terms, 'dims', scatter_dimension=1, tiled=True)  29.4 us
    gather x2, local copies, waits for them, and re-layouts, pair_products(): picked_queries = jnp.take(query_blocks, pair_ids // local_blocks, axis=0)  26.7 us
    dot_general x2, matrix products, pair_products(): jnp.einsum('gqc,gdc->gqd', picked_queries, picked_docs, preferred_element...  25.3 us
    gather x2, local copies, waits for them, and re-layouts, pair_products(): picked_docs = jnp.take(doc_side, pair_ids % local_blocks, axis=0)  18.7 us
  transfers between devices with their start and end apart: 3, of which 3 were waited for; matrix products, arithmetic and copies ran while one was open for 12% of the time, Pallas kernels for 0%

commit v1 on v0

v1 whole, which is shorter than its diff:
```python
import jax
import jax.numpy as jnp
from jax import lax
from jax.sharding import Mesh
from jax.sharding import PartitionSpec as P

D = 3072
PREFIX = 768
QB = 128
DB = 128

DOCS_PARTS = (("y", 4), ("x", 4), ("zh", 2))
DIMS_PARTS = (("zl", 4), ("c", 2))
DOCS = tuple(name for name, _ in DOCS_PARTS)
DIMS = tuple(name for name, _ in DIMS_PARTS)


def shards(queries, doc_vectors, surv_pairs, surv_count, short_pairs, short_count):
    near = lax.all_gather(queries, "zh", axis=0, tiled=True)
    every_query = lax.all_gather(near, ("y", "x"), axis=0, tiled=True)
    slice_width = queries.shape[1]
    query_blocks = every_query.reshape(-1, QB, slice_width)
    doc_blocks = doc_vectors.reshape(-1, DB, slice_width)
    local_blocks = doc_blocks.shape[0]
    columns = lax.axis_index(DIMS) * slice_width + jnp.arange(slice_width)
    prefix_blocks = jnp.where(
        columns[None, None, :] < PREFIX, doc_blocks, jnp.zeros((), doc_blocks.dtype)
    )

    def pair_products(pair_ids, doc_side):
        picked_queries = jnp.take(query_blocks, pair_ids // local_blocks, axis=0)
        picked_docs = jnp.take(doc_side, pair_ids % local_blocks, axis=0)
        return jnp.einsum(
            "gqc,gdc->gqd", picked_queries, picked_docs, preferred_element_type=jnp.float32
        )

    full_terms = pair_products(short_pairs[0], doc_blocks)
    prefix_terms = pair_products(surv_pairs[0], prefix_blocks)
    prefix_sum, full_sum = (
        lax.psum_scatter(prefix_terms, DIMS, scatter_dimension=1, tiled=True),
        lax.psum_scatter(full_terms, DIMS, scatter_dimension=1, tiled=True),
    )

    def finish(summed, live_count, factor):
        slots = jnp.arange(summed.shape[0])
        return jnp.where(slots[:, None, None] < live_count, summed * factor, jnp.float32(0.0))

    prefix_out = finish(prefix_sum, surv_count[0], float(PREFIX) ** (-0.5))
    full_out = finish(full_sum, short_count[0], float(D) ** (-0.5))
    return (prefix_out[None], full_out[None])


def solution(mesh):
    sizes = [n for _, n in DOCS_PARTS + DIMS_PARTS]
    assert mesh.devices.size == jnp.prod(jnp.array(sizes))
    parts = Mesh(mesh.devices.reshape(sizes), DOCS + DIMS)
    placed = (
        P(DOCS, DIMS),
        P(DOCS, DIMS),
        P(DOCS, None),
        P(DOCS),
        P(DOCS, None),
        P(DOCS),
    )
    return jax.shard_map(
        shards,
        mesh=parts,
        in_specs=placed,
        out_specs=(P(DOCS, None, DIMS, None), P(DOCS, None, DIMS, None)),
        check_vma=False,
    )
```

time: 421 us -> 342 us (0.81)
  waiting for transfers between devices: 329 us -> 226 us
  blocking collectives: 0 us -> 23.2 us
    all_gather x1, waiting for transfers between devices: 195 us -> 88.4 us  [shards(): every_query = lax.all_gather(near, ('y', 'x'), axis=0, tiled=True)]
    all_gather x0 -> x1, blocking collectives: none -> 23.2 us  [shards(): near = lax.all_gather(queries, 'zh', axis=0, tiled=True)]
    reduce_scatter x2, waiting for transfers between devices: 133 us -> 138 us  [the longest x1 104 us: shards(): lax.psum_scatter(prefix_terms, DIMS, scatter_dimension=1, tiled=True)]
  transfers between devices with their start and end apart: 3 -> 3, of which waited for: 3 -> 3; matrix products, arithmetic and copies ran while one was open for 12% -> 15% of each run, Pallas kernels for 0% -> 0%
where the time goes in v1:
time: 342 us
  waiting for transfers between devices  226 us (66%)
  local copies, waits for them, and re-layouts  46 us (13%)
  matrix products  25.3 us (7%)
  blocking collectives  23.2 us (7%)
  between operations  15.1 us (4%)
  other arithmetic  5.6 us (2%)
    reduce_scatter x1, waiting for transfers between devices, shards(): lax.psum_scatter(prefix_terms, DIMS, scatter_dimension=1, tiled=True)  104 us
    all_gather x1, waiting for transfers between devices, shards(): every_query = lax.all_gather(near, ('y', 'x'), axis=0, tiled=True)  88.4 us
    reduce_scatter x1, waiting for transfers between devices, shards(): lax.psum_scatter(full_terms, DIMS, scatter_dimension=1, tiled=True)  33.9 us
    gather x2, local copies, waits for them, and re-layouts, pair_products(): picked_queries = jnp.take(query_blocks, pair_ids // local_blocks, axis=0)  27.2 us
    dot_general x2, matrix products, pair_products(): jnp.einsum('gqc,gdc->gqd', picked_queries, picked_docs, preferred_element...  25.3 us
    all_gather x1, blocking collectives, shards(): near = lax.all_gather(queries, 'zh', axis=0, tiled=True)  23.2 us
    gather x2, local copies, waits for them, and re-layouts, pair_products(): picked_docs = jnp.take(doc_side, pair_ids % local_blocks, axis=0)  18.8 us
  transfers between devices with their start and end apart: 3, of which 3 were waited for; matrix products, arithmetic and copies ran while one was open for 15% of the time, Pallas kernels for 0%

profile of v1, /device:TPU:2, one launch (start us, length us, event | category | flops | bytes accessed | tf_op | source)
XLA Modules:
  0.0 341.6 jit_solution(15398356191512357973)
XLA Ops:
  7.2 0.0 all-gather.2.cloned.1.call-start
  7.2 23.2 %all_gather.6 = bf16[1024,384]{1,0:T(8,128)(2,1)} all-gather(bf16[512,384]{1,0:T(8,128)(2,1)} %param.6), channel_id=1, replica_groups=mesh['y'=4,'x'=4,'zh'=2,'zl'=4,'c'=2] {'zh'}, dimensions={0}, use_global_device_ids=true | all-gather | bytes 1179648 | tf_op jit(solution)/shard_map/all_gather | solution.py:19
  30.4 0.0 all-gather.2.cloned.1.call-update
  30.5 0.0 reduce-scatter.5.cloned.1.call-start
  30.5 0.7 fusion.12
  31.2 0.0 copy-start.2
  31.2 9.3 %gather_fusion.3 = bf16[96,128,384]{2,1,0:T(8,128)(2,1)} fusion(bf16[16,128,384]{2,1,0:T(8,128)(2,1)} %bitcast.65, s32[1024]{0:T(1024)S(1)} %get-tuple-element.10), kind=kCustom, calls=%fused_computation.3 | custom fusion | bytes 18874752 | tf_op jit(solution)/shard_map/jit(_take)/gather | solution.py:32
  40.5 0.0 copy-done.2
  40.5 88.4 %all-gather.2.cloned.1.call-done = bf16[16384,384]{1,0:T(8,128)(2,1)} async-done(((bf16[1024,384]{1,0:T(8,128)(2,1)}), bf16[16384,384]{1,0:T(8,128)(2,1)}) %all-gather.2.cloned.1.call-update) | async-done | bytes 12582928 | tf_op jit(solution)/shard_map/all_gather | solution.py:20
  128.9 12.5 %gather_fusion.2 = bf16[96,128,384]{2,1,0:T(8,128)(2,1)} fusion(bf16[128,128,384]{2,1,0:T(8,128)(2,1)} %bitcast.67, s32[1024]{0:T(1024)S(1)} %get-tuple-element.11), kind=kCustom, calls=%fused_computation.2 | custom fusion | bytes 18874752 | tf_op jit(solution)/shard_map/jit(_take)/gather | solution.py:31
  141.4 0.0 copy-start.1
  141.4 0.0 copy-start
  141.4 10.4 %fusion.5 = f32[96,128,128]{2,1,0:T(8,128)} fusion(bf16[96,128,384]{2,1,0:T(8,128)(2,1)} %gather_fusion.3, bf16[96,128,384]{2,1,0:T(8,128)(2,1)} %gather_fusion.2, pred[96]{0:T(512)(128)(4,1)S(1)} %get-tuple-element.7, pred[96]{0:T(512)(128)(4,1)S(1)} %get-tuple-element.6), kind=kOutput, calls=%fused_computation.9 | convolution fusion | flops 1217396736 | bytes 25166016 | tf_op jit(solution)/shard_map/gqc,gdc->gqd/dot_general | solution.py:33
  151.8 0.0 reduce-scatter.5.cloned.1.call-update
  151.8 0.2 reduce-scatter.3.cloned.1.call-start
  152.1 0.0 copy-done.1
  152.1 0.0 copy-done
  152.1 0.2 broadcast_select_fusion
  152.3 9.5 %gather_fusion.1 = bf16[144,128,384]{2,1,0:T(8,128)(2,1)} fusion(bf16[16,128,384]{2,1,0:T(8,128)(2,1)S(1)} %broadcast_select_fusion, s32[1024]{0:T(1024)S(1)} %pad_clamp_fusion.2), kind=kCustom, calls=%fused_computation.1 | custom fusion | bytes 28312128 | tf_op jit(solution)/shard_map/jit(_take)/gather | solution.py:32
  161.9 14.7 %gather_fusion = bf16[144,128,384]{2,1,0:T(8,128)(2,1)} fusion(bf16[128,128,384]{2,1,0:T(8,128)(2,1)} %bitcast.68, s32[1024]{0:T(1024)S(1)} %pad_clamp_fusion.3), kind=kCustom, calls=%fused_computation | custom fusion | bytes 28312128 | tf_op jit(solution)/shard_map/jit(_take)/gather | solution.py:31
  176.6 14.9 %fusion = f32[144,128,128]{2,1,0:T(8,128)} fusion(bf16[144,128,384]{2,1,0:T(8,128)(2,1)} %gather_fusion.1, bf16[144,128,384]{2,1,0:T(8,128)(2,1)} %gather_fusion, pred[144]{0:T(512)(128)(4,1)S(1)} %get-tuple-element.5, pred[144]{0:T(512)(128)(4,1)S(1)} %get-tuple-element.4), kind=kOutput, calls=%fused_computation.4 | convolution fusion | flops 1826095104 | bytes 37749024 | tf_op jit(solution)/shard_map/gqc,gdc->gqd/dot_general | solution.py:33
  191.4 0.0 reduce-scatter.3.cloned.1.call-update
  192.8 33.9 %reduce-scatter.5.cloned.1.call-done = f32[96,16,128]{2,1,0:T(8,128)} async-done(((f32[96,128,128]{2,1,0:T(8,128)}), f32[96,16,128]{2,1,0:T(8,128)}) %reduce-scatter.5.cloned.1.call-update) | async-done | bytes 786448 | tf_op jit(solution)/shard_map/reduce_scatter | solution.py:41
  226.7 2.2 select_bitcast_fusion.1
  228.9 103.7 %reduce-scatter.3.cloned.1.call-done = f32[144,16,128]{2,1,0:T(8,128)} async-done(((f32[144,128,128]{2,1,0:T(8,128)}), f32[144,16,128]{2,1,0:T(8,128)}) %reduce-scatter.3.cloned.1.call-update) | async-done | bytes 1179664 | tf_op jit(solution)/shard_map/reduce_scatter | solution.py:40
  332.6 2.5 select_bitcast_fusion
  (10 shorter events, 0.1 us)
Async XLA Ops:
  7.2 121.7 %all-gather.2.cloned.1.call-start = ((), (), s32[]{:S(2)}) async-start(), calls=%async_computation.2 | async-start | bytes 13369344 | tf_op jit(solution)/shard_map/all_gather | solution.py:20
  30.5 196.3 %reduce-scatter.5.cloned.1.call-start = ((), (), s32[]{:S(2)}) async-start(), calls=%async_computation.4 | async-start | bytes 7077888 | tf_op jit(solution)/shard_map/reduce_scatter | solution.py:41
  31.2 9.3 %copy-start.2 = (s32[1,96]{1,0:T(1,128)S(1)}, s32[1,96]{1,0:T(1,128)}, u32[]{:S(2)}) copy-start(s32[1,96]{1,0:T(1,128)} %param.10) | copy-start | bytes 1156
  141.4 10.7 %copy-start.1 = (s32[1,144]{1,0:T(1,128)S(1)}, s32[1,144]{1,0:T(1,128)}, u32[]{:S(2)}) copy-start(s32[1,144]{1,0:T(1,128)} %param.8) | copy-start | bytes 1732
  141.4 10.8 %copy-start = (bf16[2048,384]{1,0:T(8,128)(2,1)S(1)}, bf16[2048,384]{1,0:T(8,128)(2,1)}, u32[]{:S(2)}) copy-start(bf16[2048,384]{1,0:T(8,128)(2,1)} %param.7) | copy-start | bytes 4718596
  151.8 180.8 %reduce-scatter.3.cloned.1.call-start = ((), (), s32[]{:S(2)}) async-start(), calls=%async_computation.3 | async-start | bytes 10616832 | tf_op jit(solution)/shard_map/reduce_scatter | solution.py:40
Sparse Core Ops, SparseCore 0:
  30.6 98.2 all-gather.1
  151.9 74.7 reduce-scatter.4
  229.3 103.2 reduce-scatter.2

commit v2 on v1

--- a/solution.py
+++ b/solution.py
@@ -13,6 +13,24 @@
 DIMS_PARTS = (("zl", 4), ("c", 2))
 DOCS = tuple(name for name, _ in DOCS_PARTS)
 DIMS = tuple(name for name, _ in DIMS_PARTS)
+
+
+def spread_prefix(terms):
+    n_zl, n_c = (n for _, n in DIMS_PARTS)
+    slots, rows, cols = terms.shape
+    split = terms.reshape(slots, n_zl, n_c, rows // (n_zl * n_c), cols)
+    core = lax.axis_index("c")
+    kept = jnp.take(split, core, axis=2)
+    given = jnp.take(split, 1 - core, axis=2)
+    summed = kept + lax.ppermute(given, DIMS, perm=[(0, 1), (1, 0)])
+    chip = lax.axis_index("zl")
+    out = summed[:, 0]
+    for far in range(1, n_zl):
+        moved = lax.ppermute(
+            summed[:, far], DIMS, perm=[(c, far * n_c + c) for c in range(n_c)]
+        )
+        out = jnp.where(chip == far, moved, out)
+    return out
 
 
 def shards(queries, doc_vectors, surv_pairs, surv_count, short_pairs, short_count):
@@ -35,11 +53,8 @@
         )
 
     full_terms = pair_products(short_pairs[0], doc_blocks)
-    prefix_terms = pair_products(surv_pairs[0], prefix_blocks)
-    prefix_sum, full_sum = (
-        lax.psum_scatter(prefix_terms, DIMS, scatter_dimension=1, tiled=True),
-        lax.psum_scatter(full_terms, DIMS, scatter_dimension=1, tiled=True),
-    )
+    full_sum = lax.psum_scatter(full_terms, DIMS, scatter_dimension=1, tiled=True)
+    prefix_sum = spread_prefix(pair_products(surv_pairs[0], prefix_blocks))
 
     def finish(summed, live_count, factor):
         slots = jnp.arange(summed.shape[0])

time: 342 us -> 312 us (0.912)
  waiting for transfers between devices: 226 us -> 168 us
  local copies, waits for them, and re-layouts: 46 us -> 56.2 us
  starting transfers between devices: 0.3 us -> 8.98 us
  other arithmetic: 5.6 us -> 12.8 us
    reduce_scatter x1 -> x0, waiting for transfers between devices: 104 us -> none  [shards(): lax.psum_scatter(prefix_terms, DIMS, scatter_dimension=1, tiled=True)]
    ppermute x0 -> x4, waiting for transfers between devices: none -> 78.2 us  [the longest x3 69.5 us: spread_prefix(): lax.ppermute(summed[:, far], DIMS, perm=[(c, far * n_c + c) for c in rang...]
    reduce_scatter x1, waiting for transfers between devices: 33.9 us -> 0.01 us  [shards(): lax.psum_scatter(full_terms, DIMS, scatter_dimension=1, tiled=True)]
    ppermute x0 -> x4, starting transfers between devices: none -> 8.9 us  [the longest x3 6.99 us: spread_prefix(): lax.ppermute(summed[:, far], DIMS, perm=[(c, far * n_c + c) for c in rang...]
    another operation x0 -> x1, local copies, waits for them, and re-layouts: none -> 7.59 us  [spread_prefix(): kept = jnp.take(split, core, axis=2)]
    add x0 -> x1, other arithmetic: none -> 4.46 us  [spread_prefix(): summed = kept + lax.ppermute(given, DIMS, perm=[(0, 1), (1, 0)])]
  transfers between devices with their start and end apart: 3 -> 6, of which waited for: 3 -> 5; matrix products, arithmetic and copies ran while one was open for 15% -> 21% of each run, Pallas kernels for 0% -> 0%
where the time goes in v2:
time: 312 us; the launch traced here: 310 us
  waiting for transfers between devices  168 us (54%)
  local copies, waits for them, and re-layouts  56.2 us (18%)
  matrix products  25.2 us (8%)
  blocking collectives  23.3 us (7%)
  between operations  15.5 us (5%)
  other arithmetic  12.8 us (4%)
  starting transfers between devices  8.98 us (3%)
    all_gather x1, waiting for transfers between devices, shards(): every_query = lax.all_gather(near, ('y', 'x'), axis=0, tiled=True)  89.8 us
    ppermute x3, waiting for transfers between devices, spread_prefix(): lax.ppermute(summed[:, far], DIMS, perm=[(c, far * n_c + c) for c in rang...  69.5 us
    gather x2, local copies, waits for them, and re-layouts, pair_products(): picked_queries = jnp.take(query_blocks, pair_ids // local_blocks, axis=0)  27.2 us
    dot_general x2, matrix products, pair_products(): jnp.einsum('gqc,gdc->gqd', picked_queries, picked_docs, preferred_element...  25.2 us
    all_gather x1, blocking collectives, shards(): near = lax.all_gather(queries, 'zh', axis=0, tiled=True)  23.3 us
    gather x2, local copies, waits for them, and re-layouts, pair_products(): picked_docs = jnp.take(doc_side, pair_ids % local_blocks, axis=0)  17.4 us
    ppermute x1, waiting for transfers between devices, spread_prefix(): summed = kept + lax.ppermute(given, DIMS, perm=[(0, 1), (1, 0)])  8.64 us
    another operation x1, local copies, waits for them, and re-layouts, spread_prefix(): kept = jnp.take(split, core, axis=2)  7.59 us
  transfers between devices with their start and end apart: 6, of which 5 were waited for; matrix products, arithmetic and copies ran while one was open for 21% of the time, Pallas kernels for 0%

profile of v2, /device:TPU:2, one launch (start us, length us, event | category | flops | bytes accessed | tf_op | source)
XLA Modules:
  0.0 309.9 jit_solution(9384319096295745604)
XLA Ops:
  7.2 0.0 copy-start
  7.2 0.0 all-gather.2.cloned.1.call-start
  7.2 23.3 %all_gather.6 = bf16[1024,384]{1,0:T(8,128)(2,1)} all-gather(bf16[512,384]{1,0:T(8,128)(2,1)} %param.8), channel_id=1, replica_groups=mesh['y'=4,'x'=4,'zh'=2,'zl'=4,'c'=2] {'zh'}, dimensions={0}, use_global_device_ids=true | all-gather | bytes 1179648 | tf_op jit(solution)/shard_map/all_gather | solution.py:37
  30.5 0.0 all-gather.2.cloned.1.call-update
  30.6 0.0 reduce-scatter.2.cloned.1.call-start
  30.6 0.7 fusion.21
  31.3 0.0 copy-done
  31.3 0.0 copy-start.3
  31.3 7.9 %gather_fusion.3 = bf16[96,128,384]{2,1,0:T(8,128)(2,1)} fusion(bf16[16,128,384]{2,1,0:T(8,128)(2,1)S(1)} %bitcast.92, s32[1024]{0:T(1024)S(1)} %get-tuple-element.27), kind=kCustom, calls=%fused_computation.3 | custom fusion | bytes 18874752 | tf_op jit(solution)/shard_map/jit(_take)/gather | solution.py:50
  39.2 0.0 copy-done.3
  39.2 89.8 %all-gather.2.cloned.1.call-done = bf16[16384,384]{1,0:T(8,128)(2,1)} async-done(((bf16[1024,384]{1,0:T(8,128)(2,1)}), bf16[16384,384]{1,0:T(8,128)(2,1)}) %all-gather.2.cloned.1.call-update) | async-done | bytes 12582928 | tf_op jit(solution)/shard_map/all_gather | solution.py:38
  129.0 12.5 %gather_fusion.2 = bf16[96,128,384]{2,1,0:T(8,128)(2,1)} fusion(bf16[128,128,384]{2,1,0:T(8,128)(2,1)} %bitcast.94, s32[1024]{0:T(1024)S(1)} %get-tuple-element.28), kind=kCustom, calls=%fused_computation.2 | custom fusion | bytes 18874752 | tf_op jit(solution)/shard_map/jit(_take)/gather | solution.py:49
  141.5 10.3 %fusion.5 = f32[96,128,128]{2,1,0:T(8,128)} fusion(bf16[96,128,384]{2,1,0:T(8,128)(2,1)} %gather_fusion.3, bf16[96,128,384]{2,1,0:T(8,128)(2,1)} %gather_fusion.2, pred[96]{0:T(512)(128)(4,1)S(1)} %get-tuple-element.24, pred[96]{0:T(512)(128)(4,1)S(1)} %get-tuple-element.23), kind=kOutput, calls=%fused_computation.9 | convolution fusion | flops 1217396736 | bytes 25166016 | tf_op jit(solution)/shard_map/gqc,gdc->gqd/dot_general | solution.py:51
  151.8 0.0 copy-start.2
  151.8 0.0 reduce-scatter.2.cloned.1.call-update
  151.9 0.6 copy-done.2
  152.6 0.2 broadcast_select_fusion
  152.7 9.5 %gather_fusion.1 = bf16[144,128,384]{2,1,0:T(8,128)(2,1)} fusion(bf16[16,128,384]{2,1,0:T(8,128)(2,1)S(1)} %broadcast_select_fusion, s32[1024]{0:T(1024)S(1)} %pad_clamp_fusion.2), kind=kCustom, calls=%fused_computation.1 | custom fusion | bytes 28312128 | tf_op jit(solution)/shard_map/jit(_take)/gather | solution.py:50
  162.3 14.7 %gather_fusion = bf16[144,128,384]{2,1,0:T(8,128)(2,1)} fusion(bf16[128,128,384]{2,1,0:T(8,128)(2,1)} %bitcast.95, s32[1024]{0:T(1024)S(1)} %pad_clamp_fusion.3), kind=kCustom, calls=%fused_computation | custom fusion | bytes 28312128 | tf_op jit(solution)/shard_map/jit(_take)/gather | solution.py:49
  177.0 14.9 %fusion = f32[144,128,128]{2,1,0:T(8,128)} fusion(bf16[144,128,384]{2,1,0:T(8,128)(2,1)} %gather_fusion.1, bf16[144,128,384]{2,1,0:T(8,128)(2,1)} %gather_fusion, pred[144]{0:T(512)(128)(4,1)S(1)} %get-tuple-element.22, pred[144]{0:T(512)(128)(4,1)S(1)} %get-tuple-element.21), kind=kOutput, calls=%fused_computation.4 | convolution fusion | flops 1826095104 | bytes 37749024 | tf_op jit(solution)/shard_map/gqc,gdc->gqd/dot_general | solution.py:51
  191.8 7.6 %constant_dynamic-slice_fusion.1 = (f32[144,4,1,16,128]{4,3,2,1,0:T(8,128)}, f32[144,4,1,16,128]{4,3,2,1,0:T(8,128)S(1)}) fusion(f32[144,4,2,16,128]{4,3,2,1,0:T(8,128)} %bitcast.96, s32[]{:T(128)S(6)} %select_n.216, s32[]{:T(128)S(6)} %select_n.218), kind=kLoop, calls=%fused_computation.80 | loop fusion | bytes 18874376 | tf_op jit(solution)/shard_map/jit(_take) | solution.py:23
  199.4 2.7 fusion.11
  202.1 1.9 collective-permute-start
  204.0 8.6 %collective-permute-done = f32[144,4,16,128]{3,2,0,1:T(8,128)} collective-permute-done((f32[144,4,16,128]{3,2,0,1:T(8,128)}, f32[144,4,16,128]{3,2,0,1:T(8,128)}, u32[]{:S(2)}, u32[]{:S(2)}) %collective-permute-start) | collective-permute-done | bytes 4718624 | tf_op jit(solution)/shard_map/ppermute | solution.py:25
  212.7 4.5 %fusion.13 = f32[144,4,16,128]{3,2,0,1:T(8,128)S(1)} fusion(f32[144,4,16,128]{3,2,0,1:T(8,128)} %collective-permute-done, f32[144,4,1,16,128]{4,3,2,1,0:T(8,128)} %get-tuple-element.16, pred[]{:T(512)S(6)} %and.140), kind=kLoop, calls=%fused_computation.19 | loop fusion | flops 2359296 | bytes 14155777 | tf_op jit(solution)/shard_map/add | solution.py:25
  217.1 0.0 copy-start.1
  217.1 2.1 copy-done.1
  219.3 1.2 slice_bitcast_fusion.1
  220.5 2.3 collective-permute-start.3
  222.8 2.3 collective-permute-start.2
  225.2 2.3 collective-permute-start.1
  228.8 19.6 %collective-permute-done.3 = f32[144,16,128]{2,1,0:T(8,128)} collective-permute-done((f32[144,16,128]{2,1,0:T(8,128)}, f32[144,16,128]{2,1,0:T(8,128)}, u32[]{:S(2)}, u32[]{:S(2)}) %collective-permute-start.3) | collective-permute-done | bytes 1179680 | tf_op jit(solution)/shard_map/ppermute | solution.py:29
  248.4 25.2 %collective-permute-done.2 = f32[144,16,128]{2,1,0:T(8,128)} collective-permute-done((f32[144,16,128]{2,1,0:T(8,128)S(1)}, f32[144,16,128]{2,1,0:T(8,128)}, u32[]{:S(2)}, u32[]{:S(2)}) %collective-permute-start.2) | collective-permute-done | bytes 1179680 | tf_op jit(solution)/shard_map/ppermute | solution.py:29
  273.6 24.7 %collective-permute-done.1 = f32[144,16,128]{2,1,0:T(8,128)} collective-permute-done((f32[144,16,128]{2,1,0:T(8,128)S(1)}, f32[144,16,128]{2,1,0:T(8,128)}, u32[]{:S(2)}, u32[]{:S(2)}) %collective-permute-start.1) | collective-permute-done | bytes 1179680 | tf_op jit(solution)/shard_map/ppermute | solution.py:29
  298.3 2.6 fusion.20
  300.9 0.0 reduce-scatter.2.cloned.1.call-done
  300.9 2.2 select_bitcast_fusion
  (10 shorter events, 0.1 us)
Async XLA Ops:
  7.2 24.1 %copy-start = (bf16[2048,384]{1,0:T(8,128)(2,1)S(1)}, bf16[2048,384]{1,0:T(8,128)(2,1)}, u32[]{:S(2)}) copy-start(bf16[2048,384]{1,0:T(8,128)(2,1)} %param.9) | copy-start | bytes 4718596
  7.2 121.8 %all-gather.2.cloned.1.call-start = ((), (), s32[]{:S(2)}) async-start(), calls=%async_computation.1 | async-start | bytes 13369344 | tf_op jit(solution)/shard_map/all_gather | solution.py:38
  30.6 270.3 %reduce-scatter.2.cloned.1.call-start = ((), (), s32[]{:S(2)}) async-start(), calls=%async_computation.2 | async-start | bytes 7077888 | tf_op jit(solution)/shard_map/reduce_scatter | solution.py:56
  31.3 7.9 %copy-start.3 = (s32[1,96]{1,0:T(1,128)S(1)}, s32[1,96]{1,0:T(1,128)}, u32[]{:S(2)}) copy-start(s32[1,96]{1,0:T(1,128)} %param.12) | copy-start | bytes 1156
  151.8 0.7 copy-start.2
  202.1 10.6 %collective-permute-start = (f32[144,4,16,128]{3,2,0,1:T(8,128)}, f32[144,4,16,128]{3,2,0,1:T(8,128)}, u32[]{:S(2)}, u32[]{:S(2)}) collective-permute-start(f32[144,4,16,128]{3,2,0,1:T(8,128)} %fusion.11), channel_id=1, source_target_pairs={{0,1},{1,0},{8,9},{9,8},{16,17},{17,16},{24,25},{25,24},{32,33},{3... | collective-permute-start | bytes 14155784 | tf_op jit(solution)/shard_map/ppermute | solution.py:25
  217.1 2.1 copy-start.1
  220.5 27.9 %collective-permute-start.3 = (f32[144,16,128]{2,1,0:T(8,128)}, f32[144,16,128]{2,1,0:T(8,128)}, u32[]{:S(2)}, u32[]{:S(2)}) collective-permute-start(f32[144,16,128]{2,1,0:T(8,128)} %get-tuple-element.18), channel_id=1, source_target_pairs={{0,2},{1,3},{8,10},{9,11},{16,18},{17,19},{24,26},{25,27},{32,34},... | collective-permute-start | bytes 3538952 | tf_op jit(solution)/shard_map/ppermute | solution.py:29
  222.8 50.8 %collective-permute-start.2 = (f32[144,16,128]{2,1,0:T(8,128)S(1)}, f32[144,16,128]{2,1,0:T(8,128)}, u32[]{:S(2)}, u32[]{:S(2)}) collective-permute-start(f32[144,16,128]{2,1,0:T(8,128)S(1)} %get-tuple-element.19), channel_id=1, source_target_pairs={{0,4},{1,5},{8,12},{9,13},{16,20},{17,21},{24,28},{25,29},{32,36},... | collective-permute-start | bytes 3538952 | tf_op jit(solution)/shard_map/ppermute | solution.py:29
  225.2 73.2 %collective-permute-start.1 = (f32[144,16,128]{2,1,0:T(8,128)S(1)}, f32[144,16,128]{2,1,0:T(8,128)}, u32[]{:S(2)}, u32[]{:S(2)}) collective-permute-start(f32[144,16,128]{2,1,0:T(8,128)S(1)} %get-tuple-element.20), channel_id=1, source_target_pairs={{0,6},{1,7},{8,14},{9,15},{16,22},{17,23},{24,30},{25,31},{32,38},... | collective-permute-start | bytes 3538952 | tf_op jit(solution)/shard_map/ppermute | solution.py:29
Sparse Core Ops, SparseCore 0:
  30.7 98.2 all-gather.1
  152.0 74.7 reduce-scatter.1

commit v3 on v2

--- a/solution.py
+++ b/solution.py
@@ -1,6 +1,8 @@
 import jax
 import jax.numpy as jnp
 from jax import lax
+from jax.experimental import pallas as pl
+from jax.experimental.pallas import tpu as pltpu
 from jax.sharding import Mesh
 from jax.sharding import PartitionSpec as P
 
@@ -14,21 +16,75 @@
 DOCS = tuple(name for name, _ in DOCS_PARTS)
 DIMS = tuple(name for name, _ in DIMS_PARTS)
 
+GROUP = 8
 
-def spread_prefix(terms):
+
+def _pair_products(pairs, core, query_blocks, doc_blocks, split):
+    slots = pairs.shape[0]
+    n_docs, rows, width = doc_blocks.shape
     n_zl, n_c = (n for _, n in DIMS_PARTS)
-    slots, rows, cols = terms.shape
-    split = terms.reshape(slots, n_zl, n_c, rows // (n_zl * n_c), cols)
-    core = lax.axis_index("c")
-    kept = jnp.take(split, core, axis=2)
-    given = jnp.take(split, 1 - core, axis=2)
+    band = rows // (n_zl * n_c)
+
+    def query_spec(g):
+        return pl.BlockSpec(
+            (1, rows, width), lambda i, ids, me: (ids[i * GROUP + g] // n_docs, 0, 0)
+        )
+
+    def kernel(ids, me, *refs):
+        queries, docs, outs = refs[:GROUP], refs[GROUP], refs[GROUP + 1 :]
+        step = pl.program_id(0)
+        for g in range(GROUP):
+            doc = docs[ids[step * GROUP + g] % n_docs]
+            term = lax.dot_general(
+                queries[g][0], doc, (((1,), (1,)), ((), ())),
+                preferred_element_type=jnp.float32,
+            )
+            if not split:
+                outs[0][g] = term
+                continue
+            first = me[0] == 0
+            for chip in range(n_zl):
+                lo = term[(2 * chip) * band : (2 * chip + 1) * band]
+                hi = term[(2 * chip + 1) * band : (2 * chip + 2) * band]
+                outs[0][chip, g] = jnp.where(first, lo, hi)
+                outs[1][chip, g] = jnp.where(first, hi, lo)
+
+    if split:
+        part = jax.ShapeDtypeStruct((n_zl, slots, band, rows), jnp.float32)
+        out_shape = (part, part)
+        part_spec = pl.BlockSpec((n_zl, GROUP, band, rows), lambda i, ids, me: (0, i, 0, 0))
+        out_specs = (part_spec, part_spec)
+    else:
+        out_shape = (jax.ShapeDtypeStruct((slots, rows, rows), jnp.float32),)
+        out_specs = (pl.BlockSpec((GROUP, rows, rows), lambda i, ids, me: (i, 0, 0)),)
+    grid_spec = pltpu.PrefetchScalarGridSpec(
+        num_scalar_prefetch=2,
+        grid=(slots // GROUP,),
+        in_specs=[query_spec(g) for g in range(GROUP)]
+        + [pl.BlockSpec((n_docs, rows, width), lambda i, ids, me: (0, 0, 0))],
+        out_specs=out_specs,
+    )
+    cost = pl.CostEstimate(
+        flops=2 * slots * rows * rows * width,
+        transcendentals=0,
+        bytes_accessed=slots * rows * width * 2 + n_docs * rows * width * 2 + slots * rows * rows * 4,
+    )
+    return pl.pallas_call(
+        kernel,
+        out_shape=out_shape,
+        grid_spec=grid_spec,
+        compiler_params=pltpu.CompilerParams(dimension_semantics=("arbitrary",)),
+        cost_estimate=cost,
+    )(pairs, core, *([query_blocks] * GROUP), doc_blocks)
+
+
+def spread_prefix(kept, given):
+    n_zl, n_c = (n for _, n in DIMS_PARTS)
     summed = kept + lax.ppermute(given, DIMS, perm=[(0, 1), (1, 0)])
     chip = lax.axis_index("zl")
-    out = summed[:, 0]
+    out = summed[0]
     for far in range(1, n_zl):
-        moved = lax.ppermute(
-            summed[:, far], DIMS, perm=[(c, far * n_c + c) for c in range(n_c)]
-        )
+        moved = lax.ppermute(summed[far], DIMS, perm=[(c, far * n_c + c) for c in range(n_c)])
         out = jnp.where(chip == far, moved, out)
     return out
 
@@ -39,22 +95,16 @@
     slice_width = queries.shape[1]
     query_blocks = every_query.reshape(-1, QB, slice_width)
     doc_blocks = doc_vectors.reshape(-1, DB, slice_width)
-    local_blocks = doc_blocks.shape[0]
     columns = lax.axis_index(DIMS) * slice_width + jnp.arange(slice_width)
     prefix_blocks = jnp.where(
         columns[None, None, :] < PREFIX, doc_blocks, jnp.zeros((), doc_blocks.dtype)
     )
 
-    def pair_products(pair_ids, doc_side):
-        picked_queries = jnp.take(query_blocks, pair_ids // local_blocks, axis=0)
-        picked_docs = jnp.take(doc_side, pair_ids % local_blocks, axis=0)
-        return jnp.einsum(
-            "gqc,gdc->gqd", picked_queries, picked_docs, preferred_element_type=jnp.float32
-        )
-
-    full_terms = pair_products(short_pairs[0], doc_blocks)
+    core = lax.axis_index("c").astype(jnp.int32).reshape(1)
+    (full_terms,) = _pair_products(short_pairs[0], core, query_blocks, doc_blocks, False)
     full_sum = lax.psum_scatter(full_terms, DIMS, scatter_dimension=1, tiled=True)
-    prefix_sum = spread_prefix(pair_products(surv_pairs[0], prefix_blocks))
+    kept, given = _pair_products(surv_pairs[0], core, query_blocks, prefix_blocks, True)
+    prefix_sum = spread_prefix(kept, given)
 
     def finish(summed, live_count, factor):
         slots = jnp.arange(summed.shape[0])

time: 312 us -> 303 us (0.971)
  local copies, waits for them, and re-layouts: 56.2 us -> 3.48 us
  waiting for transfers between devices: 168 us -> 206 us
  Pallas kernels: 0 us -> 33.6 us
  matrix products: 25.2 us -> 0 us
  other arithmetic: 12.8 us -> 9.11 us
    gather x4 -> x0, local copies, waits for them, and re-layouts: 44.6 us -> none  [the longest x2 27.2 us: pair_products(): picked_queries = jnp.take(query_blocks, pair_ids // local_blocks, axis=0)]
    pallas_call x0 -> x2, Pallas kernels: none -> 33.6 us  [_pair_products(): pl.pallas_call(kernel, out_shape=out_shape, grid_spec=grid_spec, compiler...]
    ppermute x3, waiting for transfers between devices: 69.5 us -> 99.3 us  [spread_prefix(): lax.ppermute(summed[far], DIMS, perm=[(c, far * n_c + c) for c in range(n...]
    dot_general x2 -> x0, matrix products: 25.2 us -> none  [pair_products(): jnp.einsum('gqc,gdc->gqd', picked_queries, picked_docs, preferred_element...]
    all_gather x1, waiting for transfers between devices: 89.8 us -> 98.3 us  [shards(): every_query = lax.all_gather(near, ('y', 'x'), axis=0, tiled=True)]
    another operation x1 -> x0, local copies, waits for them, and re-layouts: 7.59 us -> none  [spread_prefix(): kept = jnp.take(split, core, axis=2)]
    select_n x4 -> x0, other arithmetic: 3.39 us -> none  [the longest x1 2.7 us: spread_prefix(): given = jnp.take(split, 1 - core, axis=2)]
  transfers between devices with their start and end apart: 6 -> 6, of which waited for: 5 -> 5; matrix products, arithmetic and copies ran while one was open for 21% -> 2% of each run, Pallas kernels for 0% -> 7%
where the time goes in v3:
time: 303 us; the launch traced here: 300 us
  waiting for transfers between devices  206 us (68%)
  Pallas kernels  33.6 us (11%)
  blocking collectives  23.2 us (8%)
  between operations  15.4 us (5%)
  other arithmetic  9.11 us (3%)
  starting transfers between devices  9.01 us (3%)
  local copies, waits for them, and re-layouts  3.48 us (1%)
    ppermute x3, waiting for transfers between devices, spread_prefix(): lax.ppermute(summed[far], DIMS, perm=[(c, far * n_c + c) for c in range(n...  99.3 us
    all_gather x1, waiting for transfers between devices, shards(): every_query = lax.all_gather(near, ('y', 'x'), axis=0, tiled=True)  98.3 us
    pallas_call x2, Pallas kernels, _pair_products(): pl.pallas_call(kernel, out_shape=out_shape, grid_spec=grid_spec, compiler...  33.6 us
    all_gather x1, blocking collectives, shards(): near = lax.all_gather(queries, 'zh', axis=0, tiled=True)  23.2 us
    ppermute x1, waiting for transfers between devices, spread_prefix(): summed = kept + lax.ppermute(given, DIMS, perm=[(0, 1), (1, 0)])  8.65 us
    ppermute x3, starting transfers between devices, spread_prefix(): lax.ppermute(summed[far], DIMS, perm=[(c, far * n_c + c) for c in range(n...  7.03 us
  transfers between devices with their start and end apart: 6, of which 5 were waited for; matrix products, arithmetic and copies ran while one was open for 2% of the time, Pallas kernels for 7%

profile of v3, /device:TPU:2, one launch (start us, length us, event | category | flops | bytes accessed | tf_op | source)
XLA Modules:
  0.0 300.2 jit_solution(9738595727966993878)
XLA Ops:
  7.2 0.0 all-gather.2.cloned.1.call-start
  7.2 23.2 %all_gather.6 = bf16[1024,384]{1,0:T(8,128)(2,1)} all-gather(bf16[512,384]{1,0:T(8,128)(2,1)} %param.6), channel_id=1, replica_groups=mesh['y'=4,'x'=4,'zh'=2,'zl'=4,'c'=2] {'zh'}, dimensions={0}, use_global_device_ids=true | all-gather | bytes 1179648 | tf_op jit(solution)/shard_map/all_gather | solution.py:93
  30.4 0.0 all-gather.2.cloned.1.call-update
  30.5 0.0 reduce-scatter.2.cloned.1.call-start
  30.5 98.3 %all-gather.2.cloned.1.call-done = bf16[16384,384]{1,0:T(8,128)(2,1)} async-done(((bf16[1024,384]{1,0:T(8,128)(2,1)}), bf16[16384,384]{1,0:T(8,128)(2,1)}) %all-gather.2.cloned.1.call-update) | async-done | bytes 12582928 | tf_op jit(solution)/shard_map/all_gather | solution.py:94
  128.9 13.9 %shard_map.78 = f32[96,128,128]{2,1,0:T(8,128)} custom-call(s32[96]{0:T(128)} %bitcast.52, s32[1]{0:T(128)} %bitcast.2.me, bf16[128,128,384]{2,1,0:T(8,128)(2,1)} %bitcast.33, bf16[128,128,384]{2,1,0:T(8,128)(2,1)} %bitcast.34, bf16[128,128,384]{2,1,0:T(8,128)(2,1)} %bitcast.35, bf16[128,128,384]{2,1,0:T(8,128)(2,1)} %bitcast.36, ...), custom_call_target="tpu_custom_call" | custom-call | flops 1207959552 | bytes 17301504 | tf_op jit(solution)/shard_map/pallas_call | solution.py:72
  142.8 0.0 copy-start.1
  142.8 0.0 reduce-scatter.2.cloned.1.call-update
  142.8 1.4 copy-done.1
  144.2 1.4 broadcast_select_fusion.refs_8_
  145.5 19.7 %shard_map.77 = (f32[4,144,16,128]{3,2,1,0:T(8,128)}, f32[4,144,16,128]{3,2,1,0:T(8,128)}) custom-call(s32[144]{0:T(256)} %bitcast.51, s32[1]{0:T(128)} %bitcast.2.me, bf16[128,128,384]{2,1,0:T(8,128)(2,1)} %bitcast.41, bf16[128,128,384]{2,1,0:T(8,128)(2,1)} %bitcast.42, bf16[128,128,384]{2,1,0:T(8,128)(2,1)} %bitcast.43, bf16[128,128,384]{2,1,0:T(8,128)(2,1)} %bitcast.44, ...), custom_call_target="tpu_custom_call" | custom-call | flops 1811939328 | bytes 25165824 | tf_op jit(solution)/shard_map/pallas_call | solution.py:72
  165.2 1.9 collective-permute-start
  167.1 8.6 %collective-permute-done = f32[4,144,16,128]{3,2,1,0:T(8,128)S(1)} collective-permute-done((f32[4,144,16,128]{3,2,1,0:T(8,128)}, f32[4,144,16,128]{3,2,1,0:T(8,128)S(1)}, u32[]{:S(2)}, u32[]{:S(2)}) %collective-permute-start) | collective-permute-done | bytes 4718624 | tf_op jit(solution)/shard_map/ppermute | solution.py:83
  175.8 3.0 add.21
  178.7 0.0 copy-start
  178.8 0.2 slice_bitcast_fusion.1
  179.0 1.9 copy-done
  180.9 2.4 collective-permute-start.1
  183.2 2.3 collective-permute-start.2
  185.6 2.3 collective-permute-start.3
  189.2 44.5 %collective-permute-done.1 = f32[144,16,128]{2,1,0:T(8,128)} collective-permute-done((f32[144,16,128]{2,1,0:T(8,128)S(1)}, f32[144,16,128]{2,1,0:T(8,128)}, u32[]{:S(2)}, u32[]{:S(2)}) %collective-permute-start.1) | collective-permute-done | bytes 1179680 | tf_op jit(solution)/shard_map/ppermute | solution.py:87
  233.8 29.7 %collective-permute-done.2 = f32[144,16,128]{2,1,0:T(8,128)} collective-permute-done((f32[144,16,128]{2,1,0:T(8,128)S(1)}, f32[144,16,128]{2,1,0:T(8,128)}, u32[]{:S(2)}, u32[]{:S(2)}) %collective-permute-start.2) | collective-permute-done | bytes 1179680 | tf_op jit(solution)/shard_map/ppermute | solution.py:87
  263.4 25.1 %collective-permute-done.3 = f32[144,16,128]{2,1,0:T(8,128)} collective-permute-done((f32[144,16,128]{2,1,0:T(8,128)S(1)}, f32[144,16,128]{2,1,0:T(8,128)}, u32[]{:S(2)}, u32[]{:S(2)}) %collective-permute-start.3) | collective-permute-done | bytes 1179680 | tf_op jit(solution)/shard_map/ppermute | solution.py:87
  288.6 2.6 fusion.5
  291.1 0.0 reduce-scatter.2.cloned.1.call-done
  291.2 2.2 select_bitcast_fusion
  (3 shorter events, 0.0 us)
Async XLA Ops:
  7.2 121.7 %all-gather.2.cloned.1.call-start = ((), (), s32[]{:S(2)}) async-start(), calls=%async_computation.1 | async-start | bytes 13369344 | tf_op jit(solution)/shard_map/all_gather | solution.py:94
  30.5 260.7 %reduce-scatter.2.cloned.1.call-start = ((), (), s32[]{:S(2)}) async-start(), calls=%async_computation.2 | async-start | bytes 7077888 | tf_op jit(solution)/shard_map/reduce_scatter | solution.py:105
  142.8 1.4 copy-start.1
  165.2 10.6 %collective-permute-start = (f32[4,144,16,128]{3,2,1,0:T(8,128)}, f32[4,144,16,128]{3,2,1,0:T(8,128)S(1)}, u32[]{:S(2)}, u32[]{:S(2)}) collective-permute-start(f32[4,144,16,128]{3,2,1,0:T(8,128)} %get-tuple-element.5), channel_id=1, source_target_pairs={{0,1},{1,0},{8,9},{9,8},{16,17},{17,16},{24,25},{25,24},{32,33},{3... | collective-permute-start | bytes 14155784 | tf_op jit(solution)/shard_map/ppermute | solution.py:83
  178.7 2.1 copy-start
  180.9 52.9 %collective-permute-start.1 = (f32[144,16,128]{2,1,0:T(8,128)S(1)}, f32[144,16,128]{2,1,0:T(8,128)}, u32[]{:S(2)}, u32[]{:S(2)}) collective-permute-start(f32[144,16,128]{2,1,0:T(8,128)S(1)} %get-tuple-element.8), channel_id=1, source_target_pairs={{0,6},{1,7},{8,14},{9,15},{16,22},{17,23},{24,30},{25,31},{32,38},... | collective-permute-start | bytes 3538952 | tf_op jit(solution)/shard_map/ppermute | solution.py:87
  183.2 80.2 %collective-permute-start.2 = (f32[144,16,128]{2,1,0:T(8,128)S(1)}, f32[144,16,128]{2,1,0:T(8,128)}, u32[]{:S(2)}, u32[]{:S(2)}) collective-permute-start(f32[144,16,128]{2,1,0:T(8,128)S(1)} %get-tuple-element.7), channel_id=1, source_target_pairs={{0,4},{1,5},{8,12},{9,13},{16,20},{17,21},{24,28},{25,29},{32,36},... | collective-permute-start | bytes 3538952 | tf_op jit(solution)/shard_map/ppermute | solution.py:87
  185.6 103.0 %collective-permute-start.3 = (f32[144,16,128]{2,1,0:T(8,128)S(1)}, f32[144,16,128]{2,1,0:T(8,128)}, u32[]{:S(2)}, u32[]{:S(2)}) collective-permute-start(f32[144,16,128]{2,1,0:T(8,128)S(1)} %get-tuple-element.6), channel_id=1, source_target_pairs={{0,2},{1,3},{8,10},{9,11},{16,18},{17,19},{24,26},{25,27},{32,34},... | collective-permute-start | bytes 3538952 | tf_op jit(solution)/shard_map/ppermute | solution.py:87
Sparse Core Ops, SparseCore 0:
  30.6 98.2 all-gather.1
  142.9 101.1 reduce-scatter.1

commit v4 on v1

v4 whole, which is shorter than its diff:
```python
import jax
import jax.numpy as jnp
from jax import lax
from jax.experimental import pallas as pl
from jax.experimental.pallas import tpu as pltpu
from jax.sharding import Mesh
from jax.sharding import PartitionSpec as P

D = 3072
PREFIX = 768
QB = 128
DB = 128

DOCS_PARTS = (("y", 4), ("x", 4), ("zh", 2))
DIMS_PARTS = (("zl", 4), ("c", 2))
DOCS = tuple(name for name, _ in DOCS_PARTS)
DIMS = tuple(name for name, _ in DIMS_PARTS)

GROUP = 8


def _slot_products(pairs, gathered, docs, prefix):
    slots = pairs.shape[0]
    _, per_shard, rows, width = gathered.shape
    n_docs = docs.shape[-3]
    local = per_shard - 1
    band = rows // (2 * local) if prefix else rows

    def spec(g, half):
        if prefix:
            return pl.BlockSpec(
                (1, 1, band, width),
                lambda i, ids: (
                    ids[i * GROUP + g] // n_docs // local,
                    local,
                    half * local + ids[i * GROUP + g] // n_docs % local,
                    0,
                ),
            )
        return pl.BlockSpec(
            (1, 1, rows, width),
            lambda i, ids: (ids[i * GROUP + g] // n_docs // local, ids[i * GROUP + g] // n_docs % local, 0, 0),
        )

    halves = 2 if prefix else 1
    dims = (((1,), (1,)), ((), ()))

    def kernel(ids, *refs):
        picked, doc_ref, out = refs[: GROUP * halves], refs[GROUP * halves], refs[-1]
        step = pl.program_id(0)
        for g in range(GROUP):
            d = ids[step * GROUP + g] % n_docs
            if prefix:
                term = lax.dot_general(
                    picked[2 * g][0, 0], doc_ref[0, d], dims, preferred_element_type=jnp.float32
                ) + lax.dot_general(
                    picked[2 * g + 1][0, 0], doc_ref[1, d], dims, preferred_element_type=jnp.float32
                )
            else:
                term = lax.dot_general(
                    picked[g][0, 0], doc_ref[d], dims, preferred_element_type=jnp.float32
                )
            out[g] = term

    in_specs = [spec(g, h) for g in range(GROUP) for h in range(halves)]
    in_specs.append(pl.BlockSpec(docs.shape, lambda i, ids: (0,) * docs.ndim))
    grid_spec = pltpu.PrefetchScalarGridSpec(
        num_scalar_prefetch=1,
        grid=(slots // GROUP,),
        in_specs=in_specs,
        out_specs=pl.BlockSpec((GROUP, band, DB), lambda i, ids: (i, 0, 0)),
    )
    cost = pl.CostEstimate(
        flops=2 * slots * band * DB * width * halves,
        transcendentals=0,
        bytes_accessed=slots * band * width * 2 * halves + docs.size * 2 + slots * band * DB * 4,
    )
    return pl.pallas_call(
        kernel,
        out_shape=jax.ShapeDtypeStruct((slots, band, DB), jnp.float32),
        grid_spec=grid_spec,
        compiler_params=pltpu.CompilerParams(dimension_semantics=("arbitrary",)),
        cost_estimate=cost,
    )(pairs, *([gathered] * (GROUP * halves)), docs)


def shards(queries, doc_vectors, surv_pairs, surv_count, short_pairs, short_count):
    n_zl, n_c = (n for _, n in DIMS_PARTS)
    n_dims = n_zl * n_c
    n_local, width = queries.shape
    local = n_local // QB
    band = QB // n_dims

    by_band = queries.reshape(local, n_dims, band, width).transpose(1, 0, 2, 3)
    spread = lax.all_to_all(by_band, DIMS, 0, 0, tiled=True)
    prefix_rows = spread[: PREFIX // width].reshape(-1, width)
    payload = jnp.concatenate([queries, prefix_rows], axis=0)
    near = lax.all_gather(payload, "zh", axis=0, tiled=True)
    gathered = lax.all_gather(near, ("y", "x"), axis=0, tiled=True)
    gathered = gathered.reshape(-1, local + 1, QB, width)

    doc_blocks = doc_vectors.reshape(-1, DB, width)
    chip = lax.axis_index("zl")
    own_half = doc_blocks
    for far in range(1, n_zl):
        moved = lax.ppermute(doc_blocks, DIMS, perm=[(c, far * n_c + c) for c in range(n_c)])
        own_half = jnp.where(chip == far, moved, own_half)
    other_half = lax.ppermute(
        own_half, DIMS, perm=[(z * n_c + c, z * n_c + 1 - c) for z in range(n_zl) for c in range(n_c)]
    )
    core = lax.axis_index("c")
    prefix_docs = jnp.where(
        core == 0, jnp.stack([own_half, other_half]), jnp.stack([other_half, own_half])
    )

    full_terms = _slot_products(short_pairs[0], gathered, doc_blocks, False)
    full_sum = lax.psum_scatter(full_terms, DIMS, scatter_dimension=1, tiled=True)
    prefix_sum = _slot_products(surv_pairs[0], gathered, prefix_docs, True)

    def finish(summed, live_count, factor):
        slots = jnp.arange(summed.shape[0])
        return jnp.where(slots[:, None, None] < live_count, summed * factor, jnp.float32(0.0))

    prefix_out = finish(prefix_sum, surv_count[0], float(PREFIX) ** (-0.5))
    full_out = finish(full_sum, short_count[0], float(D) ** (-0.5))
    return (prefix_out[None], full_out[None])


def solution(mesh):
    sizes = [n for _, n in DOCS_PARTS + DIMS_PARTS]
    assert mesh.devices.size == jnp.prod(jnp.array(sizes))
    parts = Mesh(mesh.devices.reshape(sizes), DOCS + DIMS)
    placed = (
        P(DOCS, DIMS),
        P(DOCS, DIMS),
        P(DOCS, None),
        P(DOCS),
        P(DOCS, None),
        P(DOCS),
    )
    return jax.shard_map(
        shards,
        mesh=parts,
        in_specs=placed,
        out_specs=(P(DOCS, None, DIMS, None), P(DOCS, None, DIMS, None)),
        check_vma=False,
    )
```

time: 342 us -> 394 us (1.15)
  local copies, waits for them, and re-layouts: 46 us -> 2.48 us
  Pallas kernels: 0 us -> 42.6 us
  waiting for transfers between devices: 226 us -> 267 us
  matrix products: 25.3 us -> 0 us
  blocking collectives: 23.2 us -> 46.3 us
  starting transfers between devices: 0.3 us -> 10.6 us
    ppermute x0 -> x4, waiting for transfers between devices: none -> 157 us  [the longest x3 155 us: shards(): lax.ppermute(doc_blocks, DIMS, perm=[(c, far * n_c + c) for c in range(n_...]
    reduce_scatter x1 -> x0, waiting for transfers between devices: 104 us -> none  [shards(): lax.psum_scatter(prefix_terms, DIMS, scatter_dimension=1, tiled=True)]
    gather x4 -> x0, local copies, waits for them, and re-layouts: 46 us -> none  [the longest x2 27.2 us: pair_products(): picked_queries = jnp.take(query_blocks, pair_ids // local_blocks, axis=0)]
    pallas_call x0 -> x2, Pallas kernels: none -> 42.6 us  [_slot_products(): pl.pallas_call(kernel, out_shape=jax.ShapeDtypeStruct((slots, band, DB),...]
    reduce_scatter x1, waiting for transfers between devices: 33.9 us -> 0.01 us  [shards(): lax.psum_scatter(full_terms, DIMS, scatter_dimension=1, tiled=True)]
    dot_general x2 -> x0, matrix products: 25.3 us -> none  [pair_products(): jnp.einsum('gqc,gdc->gqd', picked_queries, picked_docs, preferred_element...]
    all_gather x1, waiting for transfers between devices: 88.4 us -> 110 us  [shards(): gathered = lax.all_gather(near, ('y', 'x'), axis=0, tiled=True)]
    all_to_all x0 -> x1, blocking collectives: none -> 18.2 us  [shards(): spread = lax.all_to_all(by_band, DIMS, 0, 0, tiled=True)]
  transfers between devices with their start and end apart: 3 -> 6, of which waited for: 3 -> 5; matrix products, arithmetic and copies ran while one was open for 15% -> 1% of each run, Pallas kernels for 0% -> 7%
where the time goes in v4:
time: 394 us; the launch traced here: 391 us
  waiting for transfers between devices  267 us (68%)
  blocking collectives  46.3 us (12%)
  Pallas kernels  42.6 us (11%)
  between operations  15.4 us (4%)
  starting transfers between devices  10.6 us (3%)
  other arithmetic  7.01 us (2%)
    ppermute x3, waiting for transfers between devices, shards(): lax.ppermute(doc_blocks, DIMS, perm=[(c, far * n_c + c) for c in range(n_...  155 us
    all_gather x1, waiting for transfers between devices, shards(): gathered = lax.all_gather(near, ('y', 'x'), axis=0, tiled=True)  110 us
    pallas_call x2, Pallas kernels, _slot_products(): pl.pallas_call(kernel, out_shape=jax.ShapeDtypeStruct((slots, band, DB),...  42.6 us
    all_gather x1, blocking collectives, shards(): near = lax.all_gather(payload, 'zh', axis=0, tiled=True)  28.1 us
    all_to_all x1, blocking collectives, shards(): spread = lax.all_to_all(by_band, DIMS, 0, 0, tiled=True)  18.2 us
    ppermute x3, starting transfers between devices, shards(): lax.ppermute(doc_blocks, DIMS, perm=[(c, far * n_c + c) for c in range(n_...  10.4 us
  transfers between devices with their start and end apart: 6, of which 5 were waited for; matrix products, arithmetic and copies ran while one was open for 1% of the time, Pallas kernels for 7%

profile of v4, /device:TPU:2, one launch (start us, length us, event | category | flops | bytes accessed | tf_op | source)
XLA Modules:
  0.0 391.1 jit_solution(16680264843804980258)
XLA Ops:
  7.2 0.0 copy-start.1
  7.2 0.0 all-gather.2.cloned.1.call-start
  7.2 1.1 copy.10
  8.3 18.2 %all_to_all.5 = bf16[8,4,16,384]{3,2,1,0:T(8,128)(2,1)S(1)} all-to-all(bf16[8,4,16,384]{3,2,1,0:T(8,128)(2,1)S(1)} %bitcast.49), channel_id=1, replica_groups=mesh['y'=4,'x'=4,'zh'=2,'zl'=4,'c'=2] {'zl','c'}, dimensions={0} | all-to-all | bytes 786432 | tf_op jit(solution)/shard_map/all_to_all | solution.py:95
  26.5 0.0 copy-done.1
  26.5 0.1 pad_maximum_fusion
  26.6 28.1 %all_gather.6 = bf16[1280,384]{1,0:T(8,128)(2,1)} all-gather(bf16[640,384]{1,0:T(8,128)(2,1)S(1)} %pad_maximum_fusion), channel_id=1, replica_groups=mesh['y'=4,'x'=4,'zh'=2,'zl'=4,'c'=2] {'zh'}, dimensions={0}, use_global_device_ids=true | all-gather | bytes 1474560 | tf_op jit(solution)/shard_map/all_gather | solution.py:98
  54.7 0.0 all-gather.2.cloned.1.call-update
  54.7 0.0 reduce-scatter.2.cloned.1.call-start
  54.8 109.7 %all-gather.2.cloned.1.call-done = bf16[20480,384]{1,0:T(8,128)(2,1)} async-done(((bf16[1280,384]{1,0:T(8,128)(2,1)}), bf16[20480,384]{1,0:T(8,128)(2,1)}) %all-gather.2.cloned.1.call-update) | async-done | bytes 15728656 | tf_op jit(solution)/shard_map/all_gather | solution.py:99
  164.5 14.5 %shard_map.78 = f32[96,128,128]{2,1,0:T(8,128)} custom-call(s32[96]{0:T(128)} %bitcast.54, bf16[32,5,128,384]{3,2,1,0:T(8,128)(2,1)} %bitcast.19, bf16[32,5,128,384]{3,2,1,0:T(8,128)(2,1)} %bitcast.20, bf16[32,5,128,384]{3,2,1,0:T(8,128)(2,1)} %bitcast.21, bf16[32,5,128,384]{3,2,1,0:T(8,128)(2,1)} %bitcast.22, bf16[32,5,128,384]{3,2,1,0:T(8,128)(2,1)} %bitcast.23, ...), custom_call_target="tpu_custom_call" | custom-call | flops 1207959552 | bytes 17301504 | tf_op jit(solution)/shard_map/pallas_call | solution.py:78
  179.0 0.0 copy-start
  179.1 0.0 reduce-scatter.2.cloned.1.call-update
  179.1 1.4 copy-done
  180.5 5.5 %collective-permute-start = (bf16[16,128,384]{2,1,0:T(8,128)(2,1)S(1)}, bf16[16,128,384]{2,1,0:T(8,128)(2,1)S(1)}, u32[]{:S(2)}, u32[]{:S(2)}) collective-permute-start(bf16[16,128,384]{2,1,0:T(8,128)(2,1)S(1)} %bitcast.44), channel_id=1, source_target_pairs={{0,6},{1,7},{8,14},{9,15},{16,22},{17,23},{24,30},{25,31},{32,38},... | collective-permute-start | bytes 4718600 | tf_op jit(solution)/shard_map/ppermute | solution.py:106
  185.9 2.5 collective-permute-start.1
  188.4 2.5 collective-permute-start.2
  190.9 60.2 %collective-permute-done = bf16[16,128,384]{2,1,0:T(8,128)(2,1)S(1)} collective-permute-done((bf16[16,128,384]{2,1,0:T(8,128)(2,1)S(1)}, bf16[16,128,384]{2,1,0:T(8,128)(2,1)S(1)}, u32[]{:S(2)}, u32[]{:S(2)}) %collective-permute-start) | collective-permute-done | bytes 1572896 | tf_op jit(solution)/shard_map/ppermute | solution.py:106
  251.1 0.0 copy-start.2
  251.1 62.2 %collective-permute-done.1 = bf16[16,128,384]{2,1,0:T(8,128)(2,1)} collective-permute-done((bf16[16,128,384]{2,1,0:T(8,128)(2,1)S(1)}, bf16[16,128,384]{2,1,0:T(8,128)(2,1)}, u32[]{:S(2)}, u32[]{:S(2)}) %collective-permute-start.1) | collective-permute-done | bytes 1572896 | tf_op jit(solution)/shard_map/ppermute | solution.py:106
  313.3 0.0 copy-done.2
  313.3 32.4 %collective-permute-done.2 = bf16[16,128,384]{2,1,0:T(8,128)(2,1)} collective-permute-done((bf16[16,128,384]{2,1,0:T(8,128)(2,1)S(1)}, bf16[16,128,384]{2,1,0:T(8,128)(2,1)}, u32[]{:S(2)}, u32[]{:S(2)}) %collective-permute-start.2) | collective-permute-done | bytes 1572896 | tf_op jit(solution)/shard_map/ppermute | solution.py:106
  345.7 0.3 select_select_fusion
  346.0 0.1 collective-permute-start.3
  347.5 2.1 collective-permute-done.3
  349.5 1.9 maximum_select_fusion.refs_16_
  351.5 28.1 %shard_map.77 = f32[144,16,128]{2,1,0:T(8,128)} custom-call(s32[144]{0:T(256)} %bitcast.53, bf16[32,5,128,384]{3,2,1,0:T(8,128)(2,1)} %bitcast.30, bf16[32,5,128,384]{3,2,1,0:T(8,128)(2,1)} %bitcast.28, bf16[32,5,128,384]{3,2,1,0:T(8,128)(2,1)} %bitcast.29, bf16[32,5,128,384]{3,2,1,0:T(8,128)(2,1)} %bitcast.27, bf16[32,5,128,384]{3,2,1,0:T(8,128)(2,1)} %bitcast.31, ...), custom_call_target="tpu_custom_call" | custom-call | flops 452984832 | bytes 7864320 | tf_op jit(solution)/shard_map/pallas_call | solution.py:78
  379.5 2.5 select_bitcast_fusion
  382.0 0.0 reduce-scatter.2.cloned.1.call-done
  382.0 2.2 select_bitcast_fusion.1
  (3 shorter events, 0.0 us)
Async XLA Ops:
  7.2 19.4 %copy-start.1 = (bf16[512,384]{1,0:T(8,128)(2,1)S(1)}, bf16[512,384]{1,0:T(8,128)(2,1)}, u32[]{:S(2)}) copy-start(bf16[512,384]{1,0:T(8,128)(2,1)} %param.6) | copy-start | bytes 1179652
  7.2 157.4 %all-gather.2.cloned.1.call-start = ((), (), s32[]{:S(2)}) async-start(), calls=%async_computation.2 | async-start | bytes 16711680 | tf_op jit(solution)/shard_map/all_gather | solution.py:99
  54.7 327.3 %reduce-scatter.2.cloned.1.call-start = ((), (), s32[]{:S(2)}) async-start(), calls=%async_computation.3 | async-start | bytes 7077888 | tf_op jit(solution)/shard_map/reduce_scatter | solution.py:117
  179.0 1.4 copy-start
  180.5 70.6 %collective-permute-start = (bf16[16,128,384]{2,1,0:T(8,128)(2,1)S(1)}, bf16[16,128,384]{2,1,0:T(8,128)(2,1)S(1)}, u32[]{:S(2)}, u32[]{:S(2)}) collective-permute-start(bf16[16,128,384]{2,1,0:T(8,128)(2,1)S(1)} %bitcast.44), channel_id=1, source_target_pairs={{0,6},{1,7},{8,14},{9,15},{16,22},{17,23},{24,30},{25,31},{32,38},... | collective-permute-start | bytes 4718600 | tf_op jit(solution)/shard_map/ppermute | solution.py:106
  185.9 127.4 %collective-permute-start.1 = (bf16[16,128,384]{2,1,0:T(8,128)(2,1)S(1)}, bf16[16,128,384]{2,1,0:T(8,128)(2,1)}, u32[]{:S(2)}, u32[]{:S(2)}) collective-permute-start(bf16[16,128,384]{2,1,0:T(8,128)(2,1)S(1)} %bitcast.45), channel_id=1, source_target_pairs={{0,4},{1,5},{8,12},{9,13},{16,20},{17,21},{24,28},{25,29},{32,36},... | collective-permute-start | bytes 4718600 | tf_op jit(solution)/shard_map/ppermute | solution.py:106
  188.4 157.3 %collective-permute-start.2 = (bf16[16,128,384]{2,1,0:T(8,128)(2,1)S(1)}, bf16[16,128,384]{2,1,0:T(8,128)(2,1)}, u32[]{:S(2)}, u32[]{:S(2)}) collective-permute-start(bf16[16,128,384]{2,1,0:T(8,128)(2,1)S(1)} %bitcast.46), channel_id=1, source_target_pairs={{0,2},{1,3},{8,10},{9,11},{16,18},{17,19},{24,26},{25,27},{32,34},... | collective-permute-start | bytes 4718600 | tf_op jit(solution)/shard_map/ppermute | solution.py:106
  251.1 62.2 %copy-start.2 = (bf16[16,128,384]{2,1,0:T(8,128)(2,1)}, bf16[16,128,384]{2,1,0:T(8,128)(2,1)S(1)}, u32[]{:S(2)}) copy-start(bf16[16,128,384]{2,1,0:T(8,128)(2,1)S(1)} %collective-permute-done) | copy-start | bytes 4718596
  346.0 3.5 collective-permute-start.3
Sparse Core Ops, SparseCore 0:
  54.9 109.6 all-gather.1
  179.2 130.1 reduce-scatter.1

commit v5 on v4

--- a/solution.py
+++ b/solution.py
@@ -4,6 +4,7 @@
 from jax.experimental import pallas as pl
 from jax.experimental.pallas import tpu as pltpu
 from jax.sharding import Mesh
+
 from jax.sharding import PartitionSpec as P
 
 D = 3072
@@ -84,12 +85,19 @@
     )(pairs, *([gathered] * (GROUP * halves)), docs)
 
 
-def shards(queries, doc_vectors, surv_pairs, surv_count, short_pairs, short_count):
+def _shards(queries, doc_vectors, surv_pairs, surv_count, short_pairs, short_count):
     n_zl, n_c = (n for _, n in DIMS_PARTS)
     n_dims = n_zl * n_c
     n_local, width = queries.shape
     local = n_local // QB
     band = QB // n_dims
+
+    doc_blocks = doc_vectors.reshape(-1, DB, width)
+    chip = lax.axis_index("zl")
+    own_half = doc_blocks
+    for far in range(1, n_zl):
+        moved = lax.ppermute(doc_blocks, DIMS, perm=[(c, far * n_c + c) for c in range(n_c)])
+        own_half = jnp.where(chip == far, moved, own_half)
 
     by_band = queries.reshape(local, n_dims, band, width).transpose(1, 0, 2, 3)
     spread = lax.all_to_all(by_band, DIMS, 0, 0, tiled=True)
@@ -99,12 +107,6 @@
     gathered = lax.all_gather(near, ("y", "x"), axis=0, tiled=True)
     gathered = gathered.reshape(-1, local + 1, QB, width)
 
-    doc_blocks = doc_vectors.reshape(-1, DB, width)
-    chip = lax.axis_index("zl")
-    own_half = doc_blocks
-    for far in range(1, n_zl):
-        moved = lax.ppermute(doc_blocks, DIMS, perm=[(c, far * n_c + c) for c in range(n_c)])
-        own_half = jnp.where(chip == far, moved, own_half)
     other_half = lax.ppermute(
         own_half, DIMS, perm=[(z * n_c + c, z * n_c + 1 - c) for z in range(n_zl) for c in range(n_c)]
     )
@@ -113,8 +115,15 @@
         core == 0, jnp.stack([own_half, other_half]), jnp.stack([other_half, own_half])
     )
 
-    full_terms = _slot_products(short_pairs[0], gathered, doc_blocks, False)
-    full_sum = lax.psum_scatter(full_terms, DIMS, scatter_dimension=1, tiled=True)
+    half = short_pairs.shape[1] // 2
+    full_sum = jnp.concatenate(
+        [
+            lax.psum_scatter(
+                _slot_products(ids, gathered, doc_blocks, False), DIMS, scatter_dimension=1, tiled=True
+            )
+            for ids in (short_pairs[0, :half], short_pairs[0, half:])
+        ]
+    )
     prefix_sum = _slot_products(surv_pairs[0], gathered, prefix_docs, True)
 
     def finish(summed, live_count, factor):
@@ -139,7 +148,7 @@
         P(DOCS),
     )
     return jax.shard_map(
-        shards,
+        _shards,
         mesh=parts,
         in_specs=placed,
         out_specs=(P(DOCS, None, DIMS, None), P(DOCS, None, DIMS, None)),

time: 394 us -> 384 us (0.975)
  waiting for transfers between devices: 267 us -> 253 us
    ppermute x4, waiting for transfers between devices: 157 us -> 144 us  [the longest x3 142 us: _shards(): lax.ppermute(doc_blocks, DIMS, perm=[(c, far * n_c + c) for c in range(n_...]
    pallas_call x2 -> x3, Pallas kernels: 42.6 us -> 45.6 us  [_slot_products(): pl.pallas_call(kernel, out_shape=jax.ShapeDtypeStruct((slots, band, DB),...]
  transfers between devices with their start and end apart: 6 -> 7, of which waited for: 5 -> 5; matrix products, arithmetic and copies ran while one was open for 1% -> 1% of each run, Pallas kernels for 7% -> 10%
where the time goes in v5:
time: 384 us; the launch traced here: 381 us
  waiting for transfers between devices  253 us (66%)
  blocking collectives  46.3 us (12%)
  Pallas kernels  45.6 us (12%)
  between operations  15.1 us (4%)
  starting transfers between devices  10.7 us (3%)
  other arithmetic  6.98 us (2%)
    ppermute x3, waiting for transfers between devices, _shards(): lax.ppermute(doc_blocks, DIMS, perm=[(c, far * n_c + c) for c in range(n_...  142 us
    all_gather x1, waiting for transfers between devices, _shards(): gathered = lax.all_gather(near, ('y', 'x'), axis=0, tiled=True)  109 us
    pallas_call x3, Pallas kernels, _slot_products(): pl.pallas_call(kernel, out_shape=jax.ShapeDtypeStruct((slots, band, DB),...  45.6 us
    all_gather x1, blocking collectives, _shards(): near = lax.all_gather(payload, 'zh', axis=0, tiled=True)  28.1 us
    all_to_all x1, blocking collectives, _shards(): spread = lax.all_to_all(by_band, DIMS, 0, 0, tiled=True)  18.2 us
    ppermute x3, starting transfers between devices, _shards(): lax.ppermute(doc_blocks, DIMS, perm=[(c, far * n_c + c) for c in range(n_...  10.5 us
  transfers between devices with their start and end apart: 7, of which 5 were waited for; matrix products, arithmetic and copies ran while one was open for 1% of the time, Pallas kernels for 10%

profile of v5, /device:TPU:2, one launch (start us, length us, event | category | flops | bytes accessed | tf_op | source)
XLA Modules:
  0.0 380.9 jit_solution(14097350378028646475)
XLA Ops:
  7.2 0.0 copy-start.1
  7.2 0.0 all-gather.2.cloned.1.call-start
  7.2 1.1 copy.10
  8.3 18.2 %all_to_all.5 = bf16[8,4,16,384]{3,2,1,0:T(8,128)(2,1)S(1)} all-to-all(bf16[8,4,16,384]{3,2,1,0:T(8,128)(2,1)S(1)} %bitcast.61), channel_id=1, replica_groups=mesh['y'=4,'x'=4,'zh'=2,'zl'=4,'c'=2] {'zl','c'}, dimensions={0} | all-to-all | bytes 786432 | tf_op jit(solution)/shard_map/all_to_all | solution.py:103
  26.5 0.0 copy-done.1
  26.5 0.0 copy-start.3
  26.6 0.1 pad_maximum_fusion
  26.6 28.1 %all_gather.6 = bf16[1280,384]{1,0:T(8,128)(2,1)} all-gather(bf16[640,384]{1,0:T(8,128)(2,1)S(1)} %pad_maximum_fusion), channel_id=1, replica_groups=mesh['y'=4,'x'=4,'zh'=2,'zl'=4,'c'=2] {'zh'}, dimensions={0}, use_global_device_ids=true | all-gather | bytes 1474560 | tf_op jit(solution)/shard_map/all_gather | solution.py:106
  54.7 0.0 all-gather.2.cloned.1.call-update
  54.8 0.0 reduce-scatter.3.cloned.1.call-start
  54.8 0.0 copy-done.3
  54.8 0.6 slice_bitcast_fusion.1
  55.4 109.1 %all-gather.2.cloned.1.call-done = bf16[20480,384]{1,0:T(8,128)(2,1)} async-done(((bf16[1280,384]{1,0:T(8,128)(2,1)}), bf16[20480,384]{1,0:T(8,128)(2,1)}) %all-gather.2.cloned.1.call-update) | async-done | bytes 15728656 | tf_op jit(solution)/shard_map/all_gather | solution.py:107
  164.5 8.7 %shard_map.78 = f32[48,128,128]{2,1,0:T(8,128)} custom-call(s32[48]{0:T(128)} %get-tuple-element.2.ids, bf16[32,5,128,384]{3,2,1,0:T(8,128)(2,1)} %bitcast.22, bf16[32,5,128,384]{3,2,1,0:T(8,128)(2,1)} %bitcast.23, bf16[32,5,128,384]{3,2,1,0:T(8,128)(2,1)} %bitcast.24, bf16[32,5,128,384]{3,2,1,0:T(8,128)(2,1)} %bitcast.25, ...), custom_call_target="tpu_custom_call" | custom-call | flops 603979776 | bytes 9437184 | tf_op jit(solution)/shard_map/pallas_call | solution.py:79
  173.3 0.0 reduce-scatter.3.cloned.1.call-update
  173.3 0.0 reduce-scatter.5.cloned.1.call-start
  173.4 8.8 %shard_map.79 = f32[48,128,128]{2,1,0:T(8,128)} custom-call(s32[48]{0:T(128)} %get-tuple-element.3.ids, bf16[32,5,128,384]{3,2,1,0:T(8,128)(2,1)} %bitcast.37, bf16[32,5,128,384]{3,2,1,0:T(8,128)(2,1)} %bitcast.31, bf16[32,5,128,384]{3,2,1,0:T(8,128)(2,1)} %bitcast.32, bf16[32,5,128,384]{3,2,1,0:T(8,128)(2,1)} %bitcast.33, ...), custom_call_target="tpu_custom_call" | custom-call | flops 603979776 | bytes 9437184 | tf_op jit(solution)/shard_map/pallas_call | solution.py:79
  182.1 0.0 copy-start
  182.1 0.0 reduce-scatter.5.cloned.1.call-update
  182.2 1.4 copy-done
  183.5 5.5 %collective-permute-start = (bf16[16,128,384]{2,1,0:T(8,128)(2,1)S(1)}, bf16[16,128,384]{2,1,0:T(8,128)(2,1)S(1)}, u32[]{:S(2)}, u32[]{:S(2)}) collective-permute-start(bf16[16,128,384]{2,1,0:T(8,128)(2,1)S(1)} %bitcast.56), channel_id=1, source_target_pairs={{0,6},{1,7},{8,14},{9,15},{16,22},{17,23},{24,30},{25,31},{32,38},... | collective-permute-start | bytes 4718600 | tf_op jit(solution)/shard_map/ppermute | solution.py:99
  189.0 2.5 collective-permute-start.1
  191.5 2.5 collective-permute-start.2
  194.0 54.1 %collective-permute-done = bf16[16,128,384]{2,1,0:T(8,128)(2,1)S(1)} collective-permute-done((bf16[16,128,384]{2,1,0:T(8,128)(2,1)S(1)}, bf16[16,128,384]{2,1,0:T(8,128)(2,1)S(1)}, u32[]{:S(2)}, u32[]{:S(2)}) %collective-permute-start) | collective-permute-done | bytes 1572896 | tf_op jit(solution)/shard_map/ppermute | solution.py:99
  248.1 0.0 copy-start.2
  248.1 33.7 %collective-permute-done.1 = bf16[16,128,384]{2,1,0:T(8,128)(2,1)} collective-permute-done((bf16[16,128,384]{2,1,0:T(8,128)(2,1)S(1)}, bf16[16,128,384]{2,1,0:T(8,128)(2,1)}, u32[]{:S(2)}, u32[]{:S(2)}) %collective-permute-start.1) | collective-permute-done | bytes 1572896 | tf_op jit(solution)/shard_map/ppermute | solution.py:99
  281.8 0.0 copy-done.2
  281.8 53.9 %collective-permute-done.2 = bf16[16,128,384]{2,1,0:T(8,128)(2,1)} collective-permute-done((bf16[16,128,384]{2,1,0:T(8,128)(2,1)S(1)}, bf16[16,128,384]{2,1,0:T(8,128)(2,1)}, u32[]{:S(2)}, u32[]{:S(2)}) %collective-permute-start.2) | collective-permute-done | bytes 1572896 | tf_op jit(solution)/shard_map/ppermute | solution.py:99
  335.7 0.3 select_select_fusion
  336.0 0.1 collective-permute-start.3
  337.4 2.2 collective-permute-done.3
  339.7 1.9 maximum_select_fusion.refs_16_
  341.6 28.1 %shard_map.77 = f32[144,16,128]{2,1,0:T(8,128)} custom-call(s32[144]{0:T(256)} %bitcast.67, bf16[32,5,128,384]{3,2,1,0:T(8,128)(2,1)} %bitcast.38, bf16[32,5,128,384]{3,2,1,0:T(8,128)(2,1)} %bitcast.39, bf16[32,5,128,384]{3,2,1,0:T(8,128)(2,1)} %bitcast.40, bf16[32,5,128,384]{3,2,1,0:T(8,128)(2,1)} %bitcast.41, bf16[32,5,128,384]{3,2,1,0:T(8,128)(2,1)} %bitcast.42, ...), custom_call_target="tpu_custom_call" | custom-call | flops 452984832 | bytes 7864320 | tf_op jit(solution)/shard_map/pallas_call | solution.py:79
  369.7 2.5 select_bitcast_fusion
  372.2 0.0 reduce-scatter.3.cloned.1.call-done
  372.2 0.0 reduce-scatter.5.cloned.1.call-done
  372.2 2.2 fusion
  (3 shorter events, 0.0 us)
Async XLA Ops:
  7.2 19.4 %copy-start.1 = (bf16[512,384]{1,0:T(8,128)(2,1)S(1)}, bf16[512,384]{1,0:T(8,128)(2,1)}, u32[]{:S(2)}) copy-start(bf16[512,384]{1,0:T(8,128)(2,1)} %param.6) | copy-start | bytes 1179652
  7.2 157.4 %all-gather.2.cloned.1.call-start = ((), (), s32[]{:S(2)}) async-start(), calls=%async_computation.3 | async-start | bytes 16711680 | tf_op jit(solution)/shard_map/all_gather | solution.py:107
  26.5 28.3 %copy-start.3 = (s32[1,96]{1,0:T(1,128)S(1)}, s32[1,96]{1,0:T(1,128)}, u32[]{:S(2)}) copy-start(s32[1,96]{1,0:T(1,128)} %param.10) | copy-start | bytes 1156
  54.8 317.4 %reduce-scatter.3.cloned.1.call-start = ((), (), s32[]{:S(2)}) async-start(), calls=%async_computation.4 | async-start | bytes 3538944 | tf_op jit(solution)/shard_map/reduce_scatter | solution.py:121
  173.3 198.9 %reduce-scatter.5.cloned.1.call-start = ((), (), s32[]{:S(2)}) async-start(), calls=%async_computation.5 | async-start | bytes 3538944 | tf_op jit(solution)/shard_map/reduce_scatter | solution.py:121
  182.1 1.4 copy-start
  183.5 64.6 %collective-permute-start = (bf16[16,128,384]{2,1,0:T(8,128)(2,1)S(1)}, bf16[16,128,384]{2,1,0:T(8,128)(2,1)S(1)}, u32[]{:S(2)}, u32[]{:S(2)}) collective-permute-start(bf16[16,128,384]{2,1,0:T(8,128)(2,1)S(1)} %bitcast.56), channel_id=1, source_target_pairs={{0,6},{1,7},{8,14},{9,15},{16,22},{17,23},{24,30},{25,31},{32,38},... | collective-permute-start | bytes 4718600 | tf_op jit(solution)/shard_map/ppermute | solution.py:99
  189.0 92.8 %collective-permute-start.1 = (bf16[16,128,384]{2,1,0:T(8,128)(2,1)S(1)}, bf16[16,128,384]{2,1,0:T(8,128)(2,1)}, u32[]{:S(2)}, u32[]{:S(2)}) collective-permute-start(bf16[16,128,384]{2,1,0:T(8,128)(2,1)S(1)} %bitcast.57), channel_id=1, source_target_pairs={{0,4},{1,5},{8,12},{9,13},{16,20},{17,21},{24,28},{25,29},{32,36},... | collective-permute-start | bytes 4718600 | tf_op jit(solution)/shard_map/ppermute | solution.py:99
  191.5 144.2 %collective-permute-start.2 = (bf16[16,128,384]{2,1,0:T(8,128)(2,1)S(1)}, bf16[16,128,384]{2,1,0:T(8,128)(2,1)}, u32[]{:S(2)}, u32[]{:S(2)}) collective-permute-start(bf16[16,128,384]{2,1,0:T(8,128)(2,1)S(1)} %bitcast.58), channel_id=1, source_target_pairs={{0,2},{1,3},{8,10},{9,11},{16,18},{17,19},{24,26},{25,27},{32,34},... | collective-permute-start | bytes 4718600 | tf_op jit(solution)/shard_map/ppermute | solution.py:99
  248.1 33.7 %copy-start.2 = (bf16[16,128,384]{2,1,0:T(8,128)(2,1)}, bf16[16,128,384]{2,1,0:T(8,128)(2,1)S(1)}, u32[]{:S(2)}) copy-start(bf16[16,128,384]{2,1,0:T(8,128)(2,1)S(1)} %collective-permute-done) | copy-start | bytes 4718596
  336.0 3.6 collective-permute-start.3
Sparse Core Ops, SparseCore 0:
  54.9 109.6 all-gather.1
  173.4 67.5 reduce-scatter.2
  243.6 103.5 reduce-scatter.4

commit v6 on v5

--- a/solution.py
+++ b/solution.py
@@ -102,8 +102,16 @@
     by_band = queries.reshape(local, n_dims, band, width).transpose(1, 0, 2, 3)
     spread = lax.all_to_all(by_band, DIMS, 0, 0, tiled=True)
     prefix_rows = spread[: PREFIX // width].reshape(-1, width)
-    payload = jnp.concatenate([queries, prefix_rows], axis=0)
-    near = lax.all_gather(payload, "zh", axis=0, tiled=True)
+    near_queries = lax.all_gather(queries, "zh", axis=0, tiled=True)
+    near_rows = lax.all_gather(prefix_rows, "zh", axis=0, tiled=True)
+    n_zh = near_queries.shape[0] // n_local
+    near = jnp.concatenate(
+        [
+            part.reshape(n_zh, -1, width)
+            for part in (near_queries, near_rows)
+        ],
+        axis=1,
+    ).reshape(-1, width)
     gathered = lax.all_gather(near, ("y", "x"), axis=0, tiled=True)
     gathered = gathered.reshape(-1, local + 1, QB, width)
 
@@ -115,15 +123,8 @@
         core == 0, jnp.stack([own_half, other_half]), jnp.stack([other_half, own_half])
     )
 
-    half = short_pairs.shape[1] // 2
-    full_sum = jnp.concatenate(
-        [
-            lax.psum_scatter(
-                _slot_products(ids, gathered, doc_blocks, False), DIMS, scatter_dimension=1, tiled=True
-            )
-            for ids in (short_pairs[0, :half], short_pairs[0, half:])
-        ]
-    )
+    full_terms = _slot_products(short_pairs[0], gathered, doc_blocks, False)
+    full_sum = lax.psum_scatter(full_terms, DIMS, scatter_dimension=1, tiled=True)
     prefix_sum = _slot_products(surv_pairs[0], gathered, prefix_docs, True)
 
     def finish(summed, live_count, factor):

time: 384 us -> 396 us (1.031)
  waiting for transfers between devices: 253 us -> 266 us
  starting transfers between devices: 10.7 us -> 16.6 us
  blocking collectives: 46.3 us -> 40.7 us
    all_to_all x1 -> x0, blocking collectives: 18.2 us -> none  [_shards(): spread = lax.all_to_all(by_band, DIMS, 0, 0, tiled=True)]
    ppermute x3, waiting for transfers between devices: 142 us -> 155 us  [_shards(): lax.ppermute(doc_blocks, DIMS, perm=[(c, far * n_c + c) for c in range(n_...]
    all_gather x1 -> x2, blocking collectives: 28.1 us -> 40.7 us  [the longest x1 29.5 us: _shards(): near_queries = lax.all_gather(queries, 'zh', axis=0, tiled=True)]
    all_to_all x0 -> x1, starting transfers between devices: none -> 5.9 us  [_shards(): spread = lax.all_to_all(by_band, DIMS, 0, 0, tiled=True)]
    pallas_call x3 -> x2, Pallas kernels: 45.6 us -> 42.6 us  [_slot_products(): pl.pallas_call(kernel, out_shape=jax.ShapeDtypeStruct((slots, band, DB),...]
  transfers between devices with their start and end apart: 7 -> 7, of which waited for: 5 -> 5; matrix products, arithmetic and copies ran while one was open for 1% -> 1% of each run, Pallas kernels for 10% -> 7%
where the time goes in v6:
time: 396 us; the launch traced here: 393 us
  waiting for transfers between devices  266 us (67%)
  Pallas kernels  42.6 us (11%)
  blocking collectives  40.7 us (10%)
  starting transfers between devices  16.6 us (4%)
  between operations  15.4 us (4%)
  other arithmetic  7.99 us (2%)
    ppermute x3, waiting for transfers between devices, _shards(): lax.ppermute(doc_blocks, DIMS, perm=[(c, far * n_c + c) for c in range(n_...  155 us
    all_gather x1, waiting for transfers between devices, _shards(): gathered = lax.all_gather(near, ('y', 'x'), axis=0, tiled=True)  110 us
    pallas_call x2, Pallas kernels, _slot_products(): pl.pallas_call(kernel, out_shape=jax.ShapeDtypeStruct((slots, band, DB),...  42.6 us
    all_gather x1, blocking collectives, _shards(): near_queries = lax.all_gather(queries, 'zh', axis=0, tiled=True)  29.5 us
    all_gather x1, blocking collectives, _shards(): near_rows = lax.all_gather(prefix_rows, 'zh', axis=0, tiled=True)  11.2 us
    ppermute x3, starting transfers between devices, _shards(): lax.ppermute(doc_blocks, DIMS, perm=[(c, far * n_c + c) for c in range(n_...  10.5 us
  transfers between devices with their start and end apart: 7, of which 5 were waited for; matrix products, arithmetic and copies ran while one was open for 1% of the time, Pallas kernels for 7%

profile of v6, /device:TPU:2, one launch (start us, length us, event | category | flops | bytes accessed | tf_op | source)
XLA Modules:
  0.0 392.9 jit_solution(5214530464774086752)
XLA Ops:
  7.2 0.0 copy-start.1
  7.2 1.8 copy.9
  9.0 5.9 %all-to-all-start = ((bf16[8,4,16,384]{3,2,1,0:T(8,128)(2,1)}), bf16[8,4,16,384]{3,2,1,0:T(8,128)(2,1)S(1)}, u32[]{:S(2)}, u32[]{:S(2)}) async-start(bf16[8,4,16,384]{3,2,1,0:T(8,128)(2,1)} %copy.9), calls=%async_computation | async-start | bytes 786432 | tf_op jit(solution)/shard_map/all_to_all | solution.py:103
  14.9 0.0 all-gather.2.cloned.1.call-start
  15.0 0.0 copy-done.1
  15.0 29.5 %all_gather.9 = bf16[1024,384]{1,0:T(8,128)(2,1)S(1)} all-gather(bf16[512,384]{1,0:T(8,128)(2,1)S(1)} %copy-done.1), channel_id=1, replica_groups=mesh['y'=4,'x'=4,'zh'=2,'zl'=4,'c'=2] {'zh'}, dimensions={0}, use_global_device_ids=true | all-gather | bytes 1179648 | tf_op jit(solution)/shard_map/all_gather | solution.py:105
  44.5 0.0 all-to-all-done
  44.5 11.2 %all_gather.10 = bf16[256,384]{1,0:T(8,128)(2,1)S(1)} all-gather(bf16[128,384]{1,0:T(8,128)(2,1)S(1)} %bitcast.56), channel_id=1, replica_groups=mesh['y'=4,'x'=4,'zh'=2,'zl'=4,'c'=2] {'zh'}, dimensions={0}, use_global_device_ids=true | all-gather | bytes 294912 | tf_op jit(solution)/shard_map/all_gather | solution.py:106
  55.7 1.0 pad_maximum_fusion
  56.7 0.0 all-gather.2.cloned.1.call-update
  56.7 0.0 reduce-scatter.2.cloned.1.call-start
  56.8 109.5 %all-gather.2.cloned.1.call-done = bf16[20480,384]{1,0:T(8,128)(2,1)} async-done(((bf16[1280,384]{1,0:T(8,128)(2,1)}), bf16[20480,384]{1,0:T(8,128)(2,1)}) %all-gather.2.cloned.1.call-update) | async-done | bytes 15728656 | tf_op jit(solution)/shard_map/all_gather | solution.py:115
  166.3 14.5 %shard_map.78 = f32[96,128,128]{2,1,0:T(8,128)} custom-call(s32[96]{0:T(128)} %bitcast.58, bf16[32,5,128,384]{3,2,1,0:T(8,128)(2,1)} %bitcast.21, bf16[32,5,128,384]{3,2,1,0:T(8,128)(2,1)} %bitcast.22, bf16[32,5,128,384]{3,2,1,0:T(8,128)(2,1)} %bitcast.23, bf16[32,5,128,384]{3,2,1,0:T(8,128)(2,1)} %bitcast.24, bf16[32,5,128,384]{3,2,1,0:T(8,128)(2,1)} %bitcast.25, ...), custom_call_target="tpu_custom_call" | custom-call | flops 1207959552 | bytes 17301504 | tf_op jit(solution)/shard_map/pallas_call | solution.py:79
  180.8 0.0 copy-start
  180.8 0.0 reduce-scatter.2.cloned.1.call-update
  180.9 1.4 copy-done
  182.2 5.6 %collective-permute-start = (bf16[16,128,384]{2,1,0:T(8,128)(2,1)S(1)}, bf16[16,128,384]{2,1,0:T(8,128)(2,1)S(1)}, u32[]{:S(2)}, u32[]{:S(2)}) collective-permute-start(bf16[16,128,384]{2,1,0:T(8,128)(2,1)S(1)} %bitcast.46), channel_id=1, source_target_pairs={{0,6},{1,7},{8,14},{9,15},{16,22},{17,23},{24,30},{25,31},{32,38},... | collective-permute-start | bytes 4718600 | tf_op jit(solution)/shard_map/ppermute | solution.py:99
  187.8 2.5 collective-permute-start.1
  190.3 2.5 collective-permute-start.2
  192.8 60.1 %collective-permute-done = bf16[16,128,384]{2,1,0:T(8,128)(2,1)S(1)} collective-permute-done((bf16[16,128,384]{2,1,0:T(8,128)(2,1)S(1)}, bf16[16,128,384]{2,1,0:T(8,128)(2,1)S(1)}, u32[]{:S(2)}, u32[]{:S(2)}) %collective-permute-start) | collective-permute-done | bytes 1572896 | tf_op jit(solution)/shard_map/ppermute | solution.py:99
  252.9 0.0 copy-start.2
  252.9 62.3 %collective-permute-done.1 = bf16[16,128,384]{2,1,0:T(8,128)(2,1)} collective-permute-done((bf16[16,128,384]{2,1,0:T(8,128)(2,1)S(1)}, bf16[16,128,384]{2,1,0:T(8,128)(2,1)}, u32[]{:S(2)}, u32[]{:S(2)}) %collective-permute-start.1) | collective-permute-done | bytes 1572896 | tf_op jit(solution)/shard_map/ppermute | solution.py:99
  315.2 0.0 copy-done.2
  315.2 32.3 %collective-permute-done.2 = bf16[16,128,384]{2,1,0:T(8,128)(2,1)} collective-permute-done((bf16[16,128,384]{2,1,0:T(8,128)(2,1)S(1)}, bf16[16,128,384]{2,1,0:T(8,128)(2,1)}, u32[]{:S(2)}, u32[]{:S(2)}) %collective-permute-start.2) | collective-permute-done | bytes 1572896 | tf_op jit(solution)/shard_map/ppermute | solution.py:99
  347.5 0.3 select_select_fusion
  347.9 0.1 collective-permute-start.3
  349.3 2.1 collective-permute-done.3
  351.3 1.9 maximum_select_fusion.refs_16_
  353.3 28.1 %shard_map.77 = f32[144,16,128]{2,1,0:T(8,128)} custom-call(s32[144]{0:T(256)} %bitcast.57, bf16[32,5,128,384]{3,2,1,0:T(8,128)(2,1)} %bitcast.32, bf16[32,5,128,384]{3,2,1,0:T(8,128)(2,1)} %bitcast.30, bf16[32,5,128,384]{3,2,1,0:T(8,128)(2,1)} %bitcast.31, bf16[32,5,128,384]{3,2,1,0:T(8,128)(2,1)} %bitcast.29, bf16[32,5,128,384]{3,2,1,0:T(8,128)(2,1)} %bitcast.33, ...), custom_call_target="tpu_custom_call" | custom-call | flops 452984832 | bytes 7864320 | tf_op jit(solution)/shard_map/pallas_call | solution.py:79
  381.3 2.5 select_bitcast_fusion
  383.9 0.0 reduce-scatter.2.cloned.1.call-done
  383.9 2.2 select_bitcast_fusion.1
  (3 shorter events, 0.0 us)
Async XLA Ops:
  7.2 7.8 %copy-start.1 = (bf16[512,384]{1,0:T(8,128)(2,1)S(1)}, bf16[512,384]{1,0:T(8,128)(2,1)}, u32[]{:S(2)}) copy-start(bf16[512,384]{1,0:T(8,128)(2,1)} %param.6) | copy-start | bytes 1179652
  9.0 35.4 %all-to-all-start = ((bf16[8,4,16,384]{3,2,1,0:T(8,128)(2,1)}), bf16[8,4,16,384]{3,2,1,0:T(8,128)(2,1)S(1)}, u32[]{:S(2)}, u32[]{:S(2)}) async-start(bf16[8,4,16,384]{3,2,1,0:T(8,128)(2,1)} %copy.9), calls=%async_computation | async-start | bytes 786432 | tf_op jit(solution)/shard_map/all_to_all | solution.py:103
  14.9 151.4 %all-gather.2.cloned.1.call-start = ((), (), s32[]{:S(2)}) async-start(), calls=%async_computation.2 | async-start | bytes 16711680 | tf_op jit(solution)/shard_map/all_gather | solution.py:115
  56.7 327.1 %reduce-scatter.2.cloned.1.call-start = ((), (), s32[]{:S(2)}) async-start(), calls=%async_computation.3 | async-start | bytes 7077888 | tf_op jit(solution)/shard_map/reduce_scatter | solution.py:127
  180.8 1.4 copy-start
  182.2 70.7 %collective-permute-start = (bf16[16,128,384]{2,1,0:T(8,128)(2,1)S(1)}, bf16[16,128,384]{2,1,0:T(8,128)(2,1)S(1)}, u32[]{:S(2)}, u32[]{:S(2)}) collective-permute-start(bf16[16,128,384]{2,1,0:T(8,128)(2,1)S(1)} %bitcast.46), channel_id=1, source_target_pairs={{0,6},{1,7},{8,14},{9,15},{16,22},{17,23},{24,30},{25,31},{32,38},... | collective-permute-start | bytes 4718600 | tf_op jit(solution)/shard_map/ppermute | solution.py:99
  187.8 127.4 %collective-permute-start.1 = (bf16[16,128,384]{2,1,0:T(8,128)(2,1)S(1)}, bf16[16,128,384]{2,1,0:T(8,128)(2,1)}, u32[]{:S(2)}, u32[]{:S(2)}) collective-permute-start(bf16[16,128,384]{2,1,0:T(8,128)(2,1)S(1)} %bitcast.47), channel_id=1, source_target_pairs={{0,4},{1,5},{8,12},{9,13},{16,20},{17,21},{24,28},{25,29},{32,36},... | collective-permute-start | bytes 4718600 | tf_op jit(solution)/shard_map/ppermute | solution.py:99
  190.3 157.2 %collective-permute-start.2 = (bf16[16,128,384]{2,1,0:T(8,128)(2,1)S(1)}, bf16[16,128,384]{2,1,0:T(8,128)(2,1)}, u32[]{:S(2)}, u32[]{:S(2)}) collective-permute-start(bf16[16,128,384]{2,1,0:T(8,128)(2,1)S(1)} %bitcast.48), channel_id=1, source_target_pairs={{0,2},{1,3},{8,10},{9,11},{16,18},{17,19},{24,26},{25,27},{32,34},... | collective-permute-start | bytes 4718600 | tf_op jit(solution)/shard_map/ppermute | solution.py:99
  252.9 62.3 %copy-start.2 = (bf16[16,128,384]{2,1,0:T(8,128)(2,1)}, bf16[16,128,384]{2,1,0:T(8,128)(2,1)S(1)}, u32[]{:S(2)}) copy-start(bf16[16,128,384]{2,1,0:T(8,128)(2,1)S(1)} %collective-permute-done) | copy-start | bytes 4718596
  347.9 3.5 collective-permute-start.3
Sparse Core Ops, SparseCore 0:
  56.9 109.3 all-gather.1
  181.0 130.3 reduce-scatter.1

commit v7 on v5

--- a/solution.py
+++ b/solution.py
@@ -17,7 +17,7 @@
 DOCS = tuple(name for name, _ in DOCS_PARTS)
 DIMS = tuple(name for name, _ in DIMS_PARTS)
 
-GROUP = 8
+GROUP = 16
 
 
 def _slot_products(pairs, gathered, docs, prefix):
@@ -115,15 +115,8 @@
         core == 0, jnp.stack([own_half, other_half]), jnp.stack([other_half, own_half])
     )
 
-    half = short_pairs.shape[1] // 2
-    full_sum = jnp.concatenate(
-        [
-            lax.psum_scatter(
-                _slot_products(ids, gathered, doc_blocks, False), DIMS, scatter_dimension=1, tiled=True
-            )
-            for ids in (short_pairs[0, :half], short_pairs[0, half:])
-        ]
-    )
+    full_terms = _slot_products(short_pairs[0], gathered, doc_blocks, False)
+    full_sum = lax.psum_scatter(full_terms, DIMS, scatter_dimension=1, tiled=True)
     prefix_sum = _slot_products(surv_pairs[0], gathered, prefix_docs, True)
 
     def finish(summed, live_count, factor):

time: 384 us -> 393 us (1.023)
  waiting for transfers between devices: 253 us -> 267 us
  Pallas kernels: 45.6 us -> 41.3 us
    ppermute x3, waiting for transfers between devices: 142 us -> 155 us  [_shards(): lax.ppermute(doc_blocks, DIMS, perm=[(c, far * n_c + c) for c in range(n_...]
    pallas_call x3 -> x2, Pallas kernels: 45.6 us -> 41.3 us  [_slot_products(): pl.pallas_call(kernel, out_shape=jax.ShapeDtypeStruct((slots, band, DB),...]
  transfers between devices with their start and end apart: 7 -> 6, of which waited for: 5 -> 5; matrix products, arithmetic and copies ran while one was open for 1% -> 1% of each run, Pallas kernels for 10% -> 7%
where the time goes in v7:
time: 393 us; the launch traced here: 390 us
  waiting for transfers between devices  267 us (68%)
  blocking collectives  46.3 us (12%)
  Pallas kernels  41.3 us (11%)
  between operations  15.4 us (4%)
  starting transfers between devices  10.6 us (3%)
  other arithmetic  7.01 us (2%)
    ppermute x3, waiting for transfers between devices, _shards(): lax.ppermute(doc_blocks, DIMS, perm=[(c, far * n_c + c) for c in range(n_...  155 us
    all_gather x1, waiting for transfers between devices, _shards(): gathered = lax.all_gather(near, ('y', 'x'), axis=0, tiled=True)  110 us
    pallas_call x2, Pallas kernels, _slot_products(): pl.pallas_call(kernel, out_shape=jax.ShapeDtypeStruct((slots, band, DB),...  41.3 us
    all_gather x1, blocking collectives, _shards(): near = lax.all_gather(payload, 'zh', axis=0, tiled=True)  28.1 us
    all_to_all x1, blocking collectives, _shards(): spread = lax.all_to_all(by_band, DIMS, 0, 0, tiled=True)  18.2 us
    ppermute x3, starting transfers between devices, _shards(): lax.ppermute(doc_blocks, DIMS, perm=[(c, far * n_c + c) for c in range(n_...  10.4 us
  transfers between devices with their start and end apart: 6, of which 5 were waited for; matrix products, arithmetic and copies ran while one was open for 1% of the time, Pallas kernels for 7%

profile of v7, /device:TPU:2, one launch (start us, length us, event | category | flops | bytes accessed | tf_op | source)
XLA Modules:
  0.0 389.9 jit_solution(17611696021138498454)
XLA Ops:
  7.2 0.0 copy-start.1
  7.2 0.0 all-gather.2.cloned.1.call-start
  7.2 1.1 copy.10
  8.3 18.2 %all_to_all.5 = bf16[8,4,16,384]{3,2,1,0:T(8,128)(2,1)S(1)} all-to-all(bf16[8,4,16,384]{3,2,1,0:T(8,128)(2,1)S(1)} %bitcast.73), channel_id=1, replica_groups=mesh['y'=4,'x'=4,'zh'=2,'zl'=4,'c'=2] {'zl','c'}, dimensions={0} | all-to-all | bytes 786432 | tf_op jit(solution)/shard_map/all_to_all | solution.py:103
  26.5 0.0 copy-done.1
  26.5 0.1 pad_maximum_fusion
  26.6 28.1 %all_gather.6 = bf16[1280,384]{1,0:T(8,128)(2,1)} all-gather(bf16[640,384]{1,0:T(8,128)(2,1)S(1)} %pad_maximum_fusion), channel_id=1, replica_groups=mesh['y'=4,'x'=4,'zh'=2,'zl'=4,'c'=2] {'zh'}, dimensions={0}, use_global_device_ids=true | all-gather | bytes 1474560 | tf_op jit(solution)/shard_map/all_gather | solution.py:106
  54.7 0.0 all-gather.2.cloned.1.call-update
  54.7 0.0 reduce-scatter.2.cloned.1.call-start
  54.8 109.7 %all-gather.2.cloned.1.call-done = bf16[20480,384]{1,0:T(8,128)(2,1)} async-done(((bf16[1280,384]{1,0:T(8,128)(2,1)}), bf16[20480,384]{1,0:T(8,128)(2,1)}) %all-gather.2.cloned.1.call-update) | async-done | bytes 15728656 | tf_op jit(solution)/shard_map/all_gather | solution.py:107
  164.5 12.9 %shard_map.78 = f32[96,128,128]{2,1,0:T(8,128)} custom-call(s32[96]{0:T(128)} %bitcast.78, bf16[32,5,128,384]{3,2,1,0:T(8,128)(2,1)} %bitcast.19, bf16[32,5,128,384]{3,2,1,0:T(8,128)(2,1)} %bitcast.20, bf16[32,5,128,384]{3,2,1,0:T(8,128)(2,1)} %bitcast.21, bf16[32,5,128,384]{3,2,1,0:T(8,128)(2,1)} %bitcast.22, bf16[32,5,128,384]{3,2,1,0:T(8,128)(2,1)} %bitcast.23, ...), custom_call_target="tpu_custom_call" | custom-call | flops 1207959552 | bytes 17301504 | tf_op jit(solution)/shard_map/pallas_call | solution.py:79
  177.5 0.0 copy-start
  177.5 0.0 reduce-scatter.2.cloned.1.call-update
  177.5 1.4 copy-done
  178.9 5.5 %collective-permute-start = (bf16[16,128,384]{2,1,0:T(8,128)(2,1)S(1)}, bf16[16,128,384]{2,1,0:T(8,128)(2,1)S(1)}, u32[]{:S(2)}, u32[]{:S(2)}) collective-permute-start(bf16[16,128,384]{2,1,0:T(8,128)(2,1)S(1)} %bitcast.68), channel_id=1, source_target_pairs={{0,6},{1,7},{8,14},{9,15},{16,22},{17,23},{24,30},{25,31},{32,38},... | collective-permute-start | bytes 4718600 | tf_op jit(solution)/shard_map/ppermute | solution.py:99
  184.4 2.5 collective-permute-start.1
  186.8 2.5 collective-permute-start.2
  189.3 60.3 %collective-permute-done = bf16[16,128,384]{2,1,0:T(8,128)(2,1)S(1)} collective-permute-done((bf16[16,128,384]{2,1,0:T(8,128)(2,1)S(1)}, bf16[16,128,384]{2,1,0:T(8,128)(2,1)S(1)}, u32[]{:S(2)}, u32[]{:S(2)}) %collective-permute-start) | collective-permute-done | bytes 1572896 | tf_op jit(solution)/shard_map/ppermute | solution.py:99
  249.6 0.0 copy-start.2
  249.6 62.1 %collective-permute-done.1 = bf16[16,128,384]{2,1,0:T(8,128)(2,1)} collective-permute-done((bf16[16,128,384]{2,1,0:T(8,128)(2,1)S(1)}, bf16[16,128,384]{2,1,0:T(8,128)(2,1)}, u32[]{:S(2)}, u32[]{:S(2)}) %collective-permute-start.1) | collective-permute-done | bytes 1572896 | tf_op jit(solution)/shard_map/ppermute | solution.py:99
  311.7 0.0 copy-done.2
  311.7 32.5 %collective-permute-done.2 = bf16[16,128,384]{2,1,0:T(8,128)(2,1)} collective-permute-done((bf16[16,128,384]{2,1,0:T(8,128)(2,1)S(1)}, bf16[16,128,384]{2,1,0:T(8,128)(2,1)}, u32[]{:S(2)}, u32[]{:S(2)}) %collective-permute-start.2) | collective-permute-done | bytes 1572896 | tf_op jit(solution)/shard_map/ppermute | solution.py:99
  344.2 0.3 select_select_fusion
  344.5 0.1 collective-permute-start.3
  346.0 2.1 collective-permute-done.3
  348.0 1.9 maximum_select_fusion.refs_32_
  350.0 28.4 %shard_map.77 = f32[144,16,128]{2,1,0:T(8,128)} custom-call(s32[144]{0:T(256)} %bitcast.77, bf16[32,5,128,384]{3,2,1,0:T(8,128)(2,1)} %bitcast.42, bf16[32,5,128,384]{3,2,1,0:T(8,128)(2,1)} %bitcast.66, bf16[32,5,128,384]{3,2,1,0:T(8,128)(2,1)} %bitcast.37, bf16[32,5,128,384]{3,2,1,0:T(8,128)(2,1)} %bitcast.38, bf16[32,5,128,384]{3,2,1,0:T(8,128)(2,1)} %bitcast.39, ...), custom_call_target="tpu_custom_call" | custom-call | flops 452984832 | bytes 7864320 | tf_op jit(solution)/shard_map/pallas_call | solution.py:79
  378.4 2.5 select_bitcast_fusion
  380.9 0.0 reduce-scatter.2.cloned.1.call-done
  380.9 2.2 select_bitcast_fusion.1
  (3 shorter events, 0.0 us)
Async XLA Ops:
  7.2 19.4 %copy-start.1 = (bf16[512,384]{1,0:T(8,128)(2,1)S(1)}, bf16[512,384]{1,0:T(8,128)(2,1)}, u32[]{:S(2)}) copy-start(bf16[512,384]{1,0:T(8,128)(2,1)} %param.6) | copy-start | bytes 1179652
  7.2 157.4 %all-gather.2.cloned.1.call-start = ((), (), s32[]{:S(2)}) async-start(), calls=%async_computation.2 | async-start | bytes 16711680 | tf_op jit(solution)/shard_map/all_gather | solution.py:107
  54.7 326.1 %reduce-scatter.2.cloned.1.call-start = ((), (), s32[]{:S(2)}) async-start(), calls=%async_computation.3 | async-start | bytes 7077888 | tf_op jit(solution)/shard_map/reduce_scatter | solution.py:119
  177.5 1.4 copy-start
  178.9 70.7 %collective-permute-start = (bf16[16,128,384]{2,1,0:T(8,128)(2,1)S(1)}, bf16[16,128,384]{2,1,0:T(8,128)(2,1)S(1)}, u32[]{:S(2)}, u32[]{:S(2)}) collective-permute-start(bf16[16,128,384]{2,1,0:T(8,128)(2,1)S(1)} %bitcast.68), channel_id=1, source_target_pairs={{0,6},{1,7},{8,14},{9,15},{16,22},{17,23},{24,30},{25,31},{32,38},... | collective-permute-start | bytes 4718600 | tf_op jit(solution)/shard_map/ppermute | solution.py:99
  184.4 127.4 %collective-permute-start.1 = (bf16[16,128,384]{2,1,0:T(8,128)(2,1)S(1)}, bf16[16,128,384]{2,1,0:T(8,128)(2,1)}, u32[]{:S(2)}, u32[]{:S(2)}) collective-permute-start(bf16[16,128,384]{2,1,0:T(8,128)(2,1)S(1)} %bitcast.69), channel_id=1, source_target_pairs={{0,4},{1,5},{8,12},{9,13},{16,20},{17,21},{24,28},{25,29},{32,36},... | collective-permute-start | bytes 4718600 | tf_op jit(solution)/shard_map/ppermute | solution.py:99
  186.8 157.4 %collective-permute-start.2 = (bf16[16,128,384]{2,1,0:T(8,128)(2,1)S(1)}, bf16[16,128,384]{2,1,0:T(8,128)(2,1)}, u32[]{:S(2)}, u32[]{:S(2)}) collective-permute-start(bf16[16,128,384]{2,1,0:T(8,128)(2,1)S(1)} %bitcast.70), channel_id=1, source_target_pairs={{0,2},{1,3},{8,10},{9,11},{16,18},{17,19},{24,26},{25,27},{32,34},... | collective-permute-start | bytes 4718600 | tf_op jit(solution)/shard_map/ppermute | solution.py:99
  249.6 62.2 %copy-start.2 = (bf16[16,128,384]{2,1,0:T(8,128)(2,1)}, bf16[16,128,384]{2,1,0:T(8,128)(2,1)S(1)}, u32[]{:S(2)}) copy-start(bf16[16,128,384]{2,1,0:T(8,128)(2,1)S(1)} %collective-permute-done) | copy-start | bytes 4718596
  344.5 3.5 collective-permute-start.3
Sparse Core Ops, SparseCore 0:
  54.9 109.6 all-gather.1
  177.6 130.1 reduce-scatter.1

commit v8 on v7

--- a/solution.py
+++ b/solution.py
@@ -103,7 +103,11 @@
     spread = lax.all_to_all(by_band, DIMS, 0, 0, tiled=True)
     prefix_rows = spread[: PREFIX // width].reshape(-1, width)
     payload = jnp.concatenate([queries, prefix_rows], axis=0)
-    near = lax.all_gather(payload, "zh", axis=0, tiled=True)
+    partner = lax.ppermute(payload, "zh", perm=[(0, 1), (1, 0)])
+    low = lax.axis_index("zh") == 0
+    near = jnp.where(
+        low, jnp.concatenate([payload, partner]), jnp.concatenate([partner, payload])
+    )
     gathered = lax.all_gather(near, ("y", "x"), axis=0, tiled=True)
     gathered = gathered.reshape(-1, local + 1, QB, width)
 

time: 393 us -> 393 us (level)
  blocking collectives: 46.3 us -> 18.2 us
  waiting for transfers between devices: 267 us -> 289 us
  starting transfers between devices: 10.6 us -> 15.2 us
    all_gather x1 -> x0, blocking collectives: 28.1 us -> none  [_shards(): near = lax.all_gather(payload, 'zh', axis=0, tiled=True)]
    ppermute x0 -> x1, waiting for transfers between devices: none -> 22.9 us  [_shards(): partner = lax.ppermute(payload, 'zh', perm=[(0, 1), (1, 0)])]
    ppermute x0 -> x1, starting transfers between devices: none -> 4.58 us  [_shards(): partner = lax.ppermute(payload, 'zh', perm=[(0, 1), (1, 0)])]
  transfers between devices with their start and end apart: 6 -> 7, of which waited for: 5 -> 6; matrix products, arithmetic and copies ran while one was open for 1% -> 1% of each run, Pallas kernels for 7% -> 7%
where the time goes in v8:
time: 393 us; the launch traced here: 390 us
  waiting for transfers between devices  289 us (74%)
  Pallas kernels  41.3 us (11%)
  blocking collectives  18.2 us (5%)
  between operations  15.4 us (4%)
  starting transfers between devices  15.2 us (4%)
  other arithmetic  8.27 us (2%)
    ppermute x3, waiting for transfers between devices, _shards(): lax.ppermute(doc_blocks, DIMS, perm=[(c, far * n_c + c) for c in range(n_...  155 us
    all_gather x1, waiting for transfers between devices, _shards(): gathered = lax.all_gather(near, ('y', 'x'), axis=0, tiled=True)  110 us
    pallas_call x2, Pallas kernels, _slot_products(): pl.pallas_call(kernel, out_shape=jax.ShapeDtypeStruct((slots, band, DB),...  41.3 us
    ppermute x1, waiting for transfers between devices, _shards(): partner = lax.ppermute(payload, 'zh', perm=[(0, 1), (1, 0)])  22.9 us
    all_to_all x1, blocking collectives, _shards(): spread = lax.all_to_all(by_band, DIMS, 0, 0, tiled=True)  18.2 us
    ppermute x3, starting transfers between devices, _shards(): lax.ppermute(doc_blocks, DIMS, perm=[(c, far * n_c + c) for c in range(n_...  10.5 us
  transfers between devices with their start and end apart: 7, of which 6 were waited for; matrix products, arithmetic and copies ran while one was open for 1% of the time, Pallas kernels for 7%

profile of v8, /device:TPU:2, one launch (start us, length us, event | category | flops | bytes accessed | tf_op | source)
XLA Modules:
  0.0 390.4 jit_solution(10571223668654789740)
XLA Ops:
  7.2 0.0 copy-start.1
  7.2 0.0 all-gather.2.cloned.1.call-start
  7.2 1.1 copy.10
  8.3 18.2 %all_to_all.5 = bf16[8,4,16,384]{3,2,1,0:T(8,128)(2,1)S(1)} all-to-all(bf16[8,4,16,384]{3,2,1,0:T(8,128)(2,1)S(1)} %bitcast.74), channel_id=1, replica_groups=mesh['y'=4,'x'=4,'zh'=2,'zl'=4,'c'=2] {'zl','c'}, dimensions={0} | all-to-all | bytes 786432 | tf_op jit(solution)/shard_map/all_to_all | solution.py:103
  26.5 0.0 copy-done.1
  26.5 0.1 pad_maximum_fusion
  26.6 4.6 %collective-permute-start = (bf16[640,384]{1,0:T(8,128)(2,1)S(1)}, bf16[640,384]{1,0:T(8,128)(2,1)S(1)}, u32[]{:S(2)}, u32[]{:S(2)}) collective-permute-start(bf16[640,384]{1,0:T(8,128)(2,1)S(1)} %pad_maximum_fusion), channel_id=1, source_target_pairs={{0,8},{8,0},{1,9},{9,1},{2,10},{10,2},{3,11},{11,3},{4,12},{12,4},... | collective-permute-start | bytes 1474568 | tf_op jit(solution)/shard_map/ppermute | solution.py:106
  31.2 22.9 %collective-permute-done = bf16[640,384]{1,0:T(8,128)(2,1)S(1)} collective-permute-done((bf16[640,384]{1,0:T(8,128)(2,1)S(1)}, bf16[640,384]{1,0:T(8,128)(2,1)S(1)}, u32[]{:S(2)}, u32[]{:S(2)}) %collective-permute-start) | collective-permute-done | bytes 491552 | tf_op jit(solution)/shard_map/ppermute | solution.py:106
  54.0 1.3 maximum_select_fusion.1
  55.3 0.0 all-gather.2.cloned.1.call-update
  55.3 0.0 reduce-scatter.2.cloned.1.call-start
  55.4 109.7 %all-gather.2.cloned.1.call-done = bf16[20480,384]{1,0:T(8,128)(2,1)} async-done(((bf16[1280,384]{1,0:T(8,128)(2,1)}), bf16[20480,384]{1,0:T(8,128)(2,1)}) %all-gather.2.cloned.1.call-update) | async-done | bytes 15728656 | tf_op jit(solution)/shard_map/all_gather | solution.py:111
  165.1 13.0 %shard_map.78 = f32[96,128,128]{2,1,0:T(8,128)} custom-call(s32[96]{0:T(128)} %bitcast.79, bf16[32,5,128,384]{3,2,1,0:T(8,128)(2,1)} %bitcast.19, bf16[32,5,128,384]{3,2,1,0:T(8,128)(2,1)} %bitcast.20, bf16[32,5,128,384]{3,2,1,0:T(8,128)(2,1)} %bitcast.21, bf16[32,5,128,384]{3,2,1,0:T(8,128)(2,1)} %bitcast.22, bf16[32,5,128,384]{3,2,1,0:T(8,128)(2,1)} %bitcast.23, ...), custom_call_target="tpu_custom_call" | custom-call | flops 1207959552 | bytes 17301504 | tf_op jit(solution)/shard_map/pallas_call | solution.py:79
  178.1 0.0 copy-start
  178.1 0.0 reduce-scatter.2.cloned.1.call-update
  178.1 1.4 copy-done
  179.5 5.5 %collective-permute-start.1 = (bf16[16,128,384]{2,1,0:T(8,128)(2,1)S(1)}, bf16[16,128,384]{2,1,0:T(8,128)(2,1)S(1)}, u32[]{:S(2)}, u32[]{:S(2)}) collective-permute-start(bf16[16,128,384]{2,1,0:T(8,128)(2,1)S(1)} %bitcast.68), channel_id=1, source_target_pairs={{0,6},{1,7},{8,14},{9,15},{16,22},{17,23},{24,30},{25,31},{32,38},... | collective-permute-start | bytes 4718600 | tf_op jit(solution)/shard_map/ppermute | solution.py:99
  185.0 2.5 collective-permute-start.2
  187.5 2.5 collective-permute-start.3
  190.0 60.3 %collective-permute-done.1 = bf16[16,128,384]{2,1,0:T(8,128)(2,1)S(1)} collective-permute-done((bf16[16,128,384]{2,1,0:T(8,128)(2,1)S(1)}, bf16[16,128,384]{2,1,0:T(8,128)(2,1)S(1)}, u32[]{:S(2)}, u32[]{:S(2)}) %collective-permute-start.1) | collective-permute-done | bytes 1572896 | tf_op jit(solution)/shard_map/ppermute | solution.py:99
  250.3 0.0 copy-start.2
  250.3 62.1 %collective-permute-done.2 = bf16[16,128,384]{2,1,0:T(8,128)(2,1)} collective-permute-done((bf16[16,128,384]{2,1,0:T(8,128)(2,1)S(1)}, bf16[16,128,384]{2,1,0:T(8,128)(2,1)}, u32[]{:S(2)}, u32[]{:S(2)}) %collective-permute-start.2) | collective-permute-done | bytes 1572896 | tf_op jit(solution)/shard_map/ppermute | solution.py:99
  312.4 0.0 copy-done.2
  312.4 32.4 %collective-permute-done.3 = bf16[16,128,384]{2,1,0:T(8,128)(2,1)} collective-permute-done((bf16[16,128,384]{2,1,0:T(8,128)(2,1)S(1)}, bf16[16,128,384]{2,1,0:T(8,128)(2,1)}, u32[]{:S(2)}, u32[]{:S(2)}) %collective-permute-start.3) | collective-permute-done | bytes 1572896 | tf_op jit(solution)/shard_map/ppermute | solution.py:99
  344.7 0.3 select_select_fusion
  345.1 0.1 collective-permute-start.4
  346.5 2.1 collective-permute-done.4
  348.6 1.9 maximum_select_fusion.refs_32_
  350.5 28.4 %shard_map.77 = f32[144,16,128]{2,1,0:T(8,128)} custom-call(s32[144]{0:T(256)} %bitcast.78, bf16[32,5,128,384]{3,2,1,0:T(8,128)(2,1)} %bitcast.42, bf16[32,5,128,384]{3,2,1,0:T(8,128)(2,1)} %bitcast.66, bf16[32,5,128,384]{3,2,1,0:T(8,128)(2,1)} %bitcast.37, bf16[32,5,128,384]{3,2,1,0:T(8,128)(2,1)} %bitcast.38, bf16[32,5,128,384]{3,2,1,0:T(8,128)(2,1)} %bitcast.39, ...), custom_call_target="tpu_custom_call" | custom-call | flops 452984832 | bytes 7864320 | tf_op jit(solution)/shard_map/pallas_call | solution.py:79
  378.9 2.5 select_bitcast_fusion
  381.4 0.0 reduce-scatter.2.cloned.1.call-done
  381.4 2.2 select_bitcast_fusion.1
  (3 shorter events, 0.0 us)
Async XLA Ops:
  7.2 19.4 %copy-start.1 = (bf16[512,384]{1,0:T(8,128)(2,1)S(1)}, bf16[512,384]{1,0:T(8,128)(2,1)}, u32[]{:S(2)}) copy-start(bf16[512,384]{1,0:T(8,128)(2,1)} %param.6) | copy-start | bytes 1179652
  7.2 157.9 %all-gather.2.cloned.1.call-start = ((), (), s32[]{:S(2)}) async-start(), calls=%async_computation.2 | async-start | bytes 16711680 | tf_op jit(solution)/shard_map/all_gather | solution.py:111
  26.6 27.4 %collective-permute-start = (bf16[640,384]{1,0:T(8,128)(2,1)S(1)}, bf16[640,384]{1,0:T(8,128)(2,1)S(1)}, u32[]{:S(2)}, u32[]{:S(2)}) collective-permute-start(bf16[640,384]{1,0:T(8,128)(2,1)S(1)} %pad_maximum_fusion), channel_id=1, source_target_pairs={{0,8},{8,0},{1,9},{9,1},{2,10},{10,2},{3,11},{11,3},{4,12},{12,4},... | collective-permute-start | bytes 1474568 | tf_op jit(solution)/shard_map/ppermute | solution.py:106
  55.3 326.0 %reduce-scatter.2.cloned.1.call-start = ((), (), s32[]{:S(2)}) async-start(), calls=%async_computation.3 | async-start | bytes 7077888 | tf_op jit(solution)/shard_map/reduce_scatter | solution.py:123
  178.1 1.4 copy-start
  179.5 70.8 %collective-permute-start.1 = (bf16[16,128,384]{2,1,0:T(8,128)(2,1)S(1)}, bf16[16,128,384]{2,1,0:T(8,128)(2,1)S(1)}, u32[]{:S(2)}, u32[]{:S(2)}) collective-permute-start(bf16[16,128,384]{2,1,0:T(8,128)(2,1)S(1)} %bitcast.68), channel_id=1, source_target_pairs={{0,6},{1,7},{8,14},{9,15},{16,22},{17,23},{24,30},{25,31},{32,38},... | collective-permute-start | bytes 4718600 | tf_op jit(solution)/shard_map/ppermute | solution.py:99
  185.0 127.4 %collective-permute-start.2 = (bf16[16,128,384]{2,1,0:T(8,128)(2,1)S(1)}, bf16[16,128,384]{2,1,0:T(8,128)(2,1)}, u32[]{:S(2)}, u32[]{:S(2)}) collective-permute-start(bf16[16,128,384]{2,1,0:T(8,128)(2,1)S(1)} %bitcast.69), channel_id=1, source_target_pairs={{0,4},{1,5},{8,12},{9,13},{16,20},{17,21},{24,28},{25,29},{32,36},... | collective-permute-start | bytes 4718600 | tf_op jit(solution)/shard_map/ppermute | solution.py:99
  187.5 157.3 %collective-permute-start.3 = (bf16[16,128,384]{2,1,0:T(8,128)(2,1)S(1)}, bf16[16,128,384]{2,1,0:T(8,128)(2,1)}, u32[]{:S(2)}, u32[]{:S(2)}) collective-permute-start(bf16[16,128,384]{2,1,0:T(8,128)(2,1)S(1)} %bitcast.70), channel_id=1, source_target_pairs={{0,2},{1,3},{8,10},{9,11},{16,18},{17,19},{24,26},{25,27},{32,34},... | collective-permute-start | bytes 4718600 | tf_op jit(solution)/shard_map/ppermute | solution.py:99
  250.3 62.1 %copy-start.2 = (bf16[16,128,384]{2,1,0:T(8,128)(2,1)}, bf16[16,128,384]{2,1,0:T(8,128)(2,1)S(1)}, u32[]{:S(2)}) copy-start(bf16[16,128,384]{2,1,0:T(8,128)(2,1)S(1)} %collective-permute-done.1) | copy-start | bytes 4718596
  345.1 3.5 collective-permute-start.4
Sparse Core Ops, SparseCore 0:
  55.5 109.6 all-gather.1
  178.2 130.1 reduce-scatter.1

commit v9 on v7

--- a/solution.py
+++ b/solution.py
@@ -20,7 +20,7 @@
 GROUP = 16
 
 
-def _slot_products(pairs, gathered, docs, prefix):
+def _slot_products(pairs, gathered, docs, prefix, live=None, factor=None):
     slots = pairs.shape[0]
     _, per_shard, rows, width = gathered.shape
     n_docs = docs.shape[-3]
@@ -31,7 +31,7 @@
         if prefix:
             return pl.BlockSpec(
                 (1, 1, band, width),
-                lambda i, ids: (
+                lambda i, ids, *_: (
                     ids[i * GROUP + g] // n_docs // local,
                     local,
                     half * local + ids[i * GROUP + g] // n_docs % local,
@@ -40,13 +40,17 @@
             )
         return pl.BlockSpec(
             (1, 1, rows, width),
-            lambda i, ids: (ids[i * GROUP + g] // n_docs // local, ids[i * GROUP + g] // n_docs % local, 0, 0),
+            lambda i, ids, *_: (ids[i * GROUP + g] // n_docs // local, ids[i * GROUP + g] // n_docs % local, 0, 0),
         )
 
     halves = 2 if prefix else 1
     dims = (((1,), (1,)), ((), ()))
 
+    scalars = 1 if live is None else 2
+
     def kernel(ids, *refs):
+        live_ref = refs[0] if live is not None else None
+        refs = refs[scalars - 1 :]
         picked, doc_ref, out = refs[: GROUP * halves], refs[GROUP * halves], refs[-1]
         step = pl.program_id(0)
         for g in range(GROUP):
@@ -61,15 +65,18 @@
                 term = lax.dot_general(
                     picked[g][0, 0], doc_ref[d], dims, preferred_element_type=jnp.float32
                 )
+            if live is not None:
+                slot = step * GROUP + g
+                term = jnp.where(slot < live_ref[0], term * factor, jnp.zeros_like(term))
             out[g] = term
 
     in_specs = [spec(g, h) for g in range(GROUP) for h in range(halves)]
-    in_specs.append(pl.BlockSpec(docs.shape, lambda i, ids: (0,) * docs.ndim))
+    in_specs.append(pl.BlockSpec(docs.shape, lambda i, ids, *_: (0,) * docs.ndim))
     grid_spec = pltpu.PrefetchScalarGridSpec(
-        num_scalar_prefetch=1,
+        num_scalar_prefetch=scalars,
         grid=(slots // GROUP,),
         in_specs=in_specs,
-        out_specs=pl.BlockSpec((GROUP, band, DB), lambda i, ids: (i, 0, 0)),
+        out_specs=pl.BlockSpec((GROUP, band, DB), lambda i, ids, *_: (i, 0, 0)),
     )
     cost = pl.CostEstimate(
         flops=2 * slots * band * DB * width * halves,
@@ -82,7 +89,7 @@
         grid_spec=grid_spec,
         compiler_params=pltpu.CompilerParams(dimension_semantics=("arbitrary",)),
         cost_estimate=cost,
-    )(pairs, *([gathered] * (GROUP * halves)), docs)
+    )(pairs, *(() if live is None else (live,)), *([gathered] * (GROUP * halves)), docs)
 
 
 def _shards(queries, doc_vectors, surv_pairs, surv_count, short_pairs, short_count):
@@ -115,8 +122,10 @@
         core == 0, jnp.stack([own_half, other_half]), jnp.stack([other_half, own_half])
     )
 
-    full_terms = _slot_products(short_pairs[0], gathered, doc_blocks, False)
-    full_sum = lax.psum_scatter(full_terms, DIMS, scatter_dimension=1, tiled=True)
+    full_terms = _slot_products(
+        short_pairs[0], gathered, doc_blocks, False, short_count, float(D) ** (-0.5)
+    )
+    full_out = lax.psum_scatter(full_terms, DIMS, scatter_dimension=1, tiled=True)
     prefix_sum = _slot_products(surv_pairs[0], gathered, prefix_docs, True)
 
     def finish(summed, live_count, factor):
@@ -124,7 +133,6 @@
         return jnp.where(slots[:, None, None] < live_count, summed * factor, jnp.float32(0.0))
 
     prefix_out = finish(prefix_sum, surv_count[0], float(PREFIX) ** (-0.5))
-    full_out = finish(full_sum, short_count[0], float(D) ** (-0.5))
     return (prefix_out[None], full_out[None])
 
 

time: 393 us -> 390 us (level)
  no operation moved by 1% of the time
where the time goes in v9:
time: 390 us; the launch traced here: 388 us
  waiting for transfers between devices  267 us (68%)
  blocking collectives  46.3 us (12%)
  Pallas kernels  41.3 us (11%)
  between operations  15.4 us (4%)
  starting transfers between devices  10.7 us (3%)
  other arithmetic  4.82 us (1%)
    ppermute x3, waiting for transfers between devices, _shards(): lax.ppermute(doc_blocks, DIMS, perm=[(c, far * n_c + c) for c in range(n_...  155 us
    all_gather x1, waiting for transfers between devices, _shards(): gathered = lax.all_gather(near, ('y', 'x'), axis=0, tiled=True)  109 us
    pallas_call x2, Pallas kernels, _slot_products(): pl.pallas_call(kernel, out_shape=jax.ShapeDtypeStruct((slots, band, DB),...  41.3 us
    all_gather x1, blocking collectives, _shards(): near = lax.all_gather(payload, 'zh', axis=0, tiled=True)  28.1 us
    all_to_all x1, blocking collectives, _shards(): spread = lax.all_to_all(by_band, DIMS, 0, 0, tiled=True)  18.2 us
    ppermute x3, starting transfers between devices, _shards(): lax.ppermute(doc_blocks, DIMS, perm=[(c, far * n_c + c) for c in range(n_...  10.5 us
  transfers between devices with their start and end apart: 6, of which 5 were waited for; matrix products, arithmetic and copies ran while one was open for 1% of the time, Pallas kernels for 7%

profile of v9, /device:TPU:2, one launch (start us, length us, event | category | flops | bytes accessed | tf_op | source)
XLA Modules:
  0.0 387.7 jit_solution(15823363246388901528)
XLA Ops:
  7.2 0.0 copy-start.1
  7.2 0.0 all-gather.2.cloned.1.call-start
  7.2 1.1 copy.10
  8.3 18.2 %all_to_all.5 = bf16[8,4,16,384]{3,2,1,0:T(8,128)(2,1)S(1)} all-to-all(bf16[8,4,16,384]{3,2,1,0:T(8,128)(2,1)S(1)} %bitcast.70), channel_id=1, replica_groups=mesh['y'=4,'x'=4,'zh'=2,'zl'=4,'c'=2] {'zl','c'}, dimensions={0} | all-to-all | bytes 786432 | tf_op jit(solution)/shard_map/all_to_all | solution.py:110
  26.5 0.0 copy-done.1
  26.5 0.1 pad_maximum_fusion
  26.6 28.1 %all_gather.6 = bf16[1280,384]{1,0:T(8,128)(2,1)} all-gather(bf16[640,384]{1,0:T(8,128)(2,1)S(1)} %pad_maximum_fusion), channel_id=1, replica_groups=mesh['y'=4,'x'=4,'zh'=2,'zl'=4,'c'=2] {'zh'}, dimensions={0}, use_global_device_ids=true | all-gather | bytes 1474560 | tf_op jit(solution)/shard_map/all_gather | solution.py:113
  54.7 0.0 all-gather.2.cloned.1.call-update
  54.7 0.0 reduce-scatter.2.cloned.1.call-start
  55.4 109.1 %all-gather.2.cloned.1.call-done = bf16[20480,384]{1,0:T(8,128)(2,1)} async-done(((bf16[1280,384]{1,0:T(8,128)(2,1)}), bf16[20480,384]{1,0:T(8,128)(2,1)}) %all-gather.2.cloned.1.call-update) | async-done | bytes 15728656 | tf_op jit(solution)/shard_map/all_gather | solution.py:114
  164.5 13.0 %shard_map.78 = f32[96,128,128]{2,1,0:T(8,128)} custom-call(s32[96]{0:T(128)} %bitcast.75, s32[1]{0:T(128)S(6)} %copy.12.refs_0_, bf16[32,5,128,384]{3,2,1,0:T(8,128)(2,1)} %bitcast.16, bf16[32,5,128,384]{3,2,1,0:T(8,128)(2,1)} %bitcast.17, bf16[32,5,128,384]{3,2,1,0:T(8,128)(2,1)} %bitcast.18, bf16[32,5,128,384]{3,2,1,0:T(8,128)(2,1)} %bitcast.19, ...), custom_call_target="tpu_custom_call" | custom-call | flops 1207959552 | bytes 17301504 | tf_op jit(solution)/shard_map/pallas_call | solution.py:86
  177.5 0.0 copy-start
  177.5 0.0 reduce-scatter.2.cloned.1.call-update
  177.5 1.4 copy-done
  178.9 5.5 %collective-permute-start = (bf16[16,128,384]{2,1,0:T(8,128)(2,1)S(1)}, bf16[16,128,384]{2,1,0:T(8,128)(2,1)S(1)}, u32[]{:S(2)}, u32[]{:S(2)}) collective-permute-start(bf16[16,128,384]{2,1,0:T(8,128)(2,1)S(1)} %bitcast.65), channel_id=1, source_target_pairs={{0,6},{1,7},{8,14},{9,15},{16,22},{17,23},{24,30},{25,31},{32,38},... | collective-permute-start | bytes 4718600 | tf_op jit(solution)/shard_map/ppermute | solution.py:106
  184.4 2.5 collective-permute-start.1
  186.9 2.5 collective-permute-start.2
  189.4 60.3 %collective-permute-done = bf16[16,128,384]{2,1,0:T(8,128)(2,1)S(1)} collective-permute-done((bf16[16,128,384]{2,1,0:T(8,128)(2,1)S(1)}, bf16[16,128,384]{2,1,0:T(8,128)(2,1)S(1)}, u32[]{:S(2)}, u32[]{:S(2)}) %collective-permute-start) | collective-permute-done | bytes 1572896 | tf_op jit(solution)/shard_map/ppermute | solution.py:106
  249.6 0.0 copy-start.2
  249.6 62.1 %collective-permute-done.1 = bf16[16,128,384]{2,1,0:T(8,128)(2,1)} collective-permute-done((bf16[16,128,384]{2,1,0:T(8,128)(2,1)S(1)}, bf16[16,128,384]{2,1,0:T(8,128)(2,1)}, u32[]{:S(2)}, u32[]{:S(2)}) %collective-permute-start.1) | collective-permute-done | bytes 1572896 | tf_op jit(solution)/shard_map/ppermute | solution.py:106
  311.8 0.0 copy-done.2
  311.8 32.4 %collective-permute-done.2 = bf16[16,128,384]{2,1,0:T(8,128)(2,1)} collective-permute-done((bf16[16,128,384]{2,1,0:T(8,128)(2,1)S(1)}, bf16[16,128,384]{2,1,0:T(8,128)(2,1)}, u32[]{:S(2)}, u32[]{:S(2)}) %collective-permute-start.2) | collective-permute-done | bytes 1572896 | tf_op jit(solution)/shard_map/ppermute | solution.py:106
  344.2 0.3 select_select_fusion
  344.5 0.1 collective-permute-start.3
  345.3 2.7 collective-permute-done.3
  348.0 1.9 maximum_select_fusion.refs_32_
  349.9 28.4 %shard_map.77 = f32[144,16,128]{2,1,0:T(8,128)} custom-call(s32[144]{0:T(256)} %bitcast.74, bf16[32,5,128,384]{3,2,1,0:T(8,128)(2,1)} %bitcast.39, bf16[32,5,128,384]{3,2,1,0:T(8,128)(2,1)} %bitcast.63, bf16[32,5,128,384]{3,2,1,0:T(8,128)(2,1)} %bitcast.34, bf16[32,5,128,384]{3,2,1,0:T(8,128)(2,1)} %bitcast.35, bf16[32,5,128,384]{3,2,1,0:T(8,128)(2,1)} %bitcast.36, ...), custom_call_target="tpu_custom_call" | custom-call | flops 452984832 | bytes 7864320 | tf_op jit(solution)/shard_map/pallas_call | solution.py:86
  378.3 2.5 select_bitcast_fusion
  380.8 0.0 reduce-scatter.2.cloned.1.call-done
  (2 shorter events, 0.0 us)
Async XLA Ops:
  7.2 19.4 %copy-start.1 = (bf16[512,384]{1,0:T(8,128)(2,1)S(1)}, bf16[512,384]{1,0:T(8,128)(2,1)}, u32[]{:S(2)}) copy-start(bf16[512,384]{1,0:T(8,128)(2,1)} %param.6) | copy-start | bytes 1179652
  7.2 157.4 %all-gather.2.cloned.1.call-start = ((), (), s32[]{:S(2)}) async-start(), calls=%async_computation.2 | async-start | bytes 16711680 | tf_op jit(solution)/shard_map/all_gather | solution.py:114
  54.7 326.1 %reduce-scatter.2.cloned.1.call-start = ((), (), s32[]{:S(2)}) async-start(), calls=%async_computation.3 | async-start | bytes 7077888 | tf_op jit(solution)/shard_map/reduce_scatter | solution.py:128
  177.5 1.4 copy-start
  178.9 70.7 %collective-permute-start = (bf16[16,128,384]{2,1,0:T(8,128)(2,1)S(1)}, bf16[16,128,384]{2,1,0:T(8,128)(2,1)S(1)}, u32[]{:S(2)}, u32[]{:S(2)}) collective-permute-start(bf16[16,128,384]{2,1,0:T(8,128)(2,1)S(1)} %bitcast.65), channel_id=1, source_target_pairs={{0,6},{1,7},{8,14},{9,15},{16,22},{17,23},{24,30},{25,31},{32,38},... | collective-permute-start | bytes 4718600 | tf_op jit(solution)/shard_map/ppermute | solution.py:106
  184.4 127.4 %collective-permute-start.1 = (bf16[16,128,384]{2,1,0:T(8,128)(2,1)S(1)}, bf16[16,128,384]{2,1,0:T(8,128)(2,1)}, u32[]{:S(2)}, u32[]{:S(2)}) collective-permute-start(bf16[16,128,384]{2,1,0:T(8,128)(2,1)S(1)} %bitcast.66), channel_id=1, source_target_pairs={{0,4},{1,5},{8,12},{9,13},{16,20},{17,21},{24,28},{25,29},{32,36},... | collective-permute-start | bytes 4718600 | tf_op jit(solution)/shard_map/ppermute | solution.py:106
  186.9 157.3 %collective-permute-start.2 = (bf16[16,128,384]{2,1,0:T(8,128)(2,1)S(1)}, bf16[16,128,384]{2,1,0:T(8,128)(2,1)}, u32[]{:S(2)}, u32[]{:S(2)}) collective-permute-start(bf16[16,128,384]{2,1,0:T(8,128)(2,1)S(1)} %bitcast.67), channel_id=1, source_target_pairs={{0,2},{1,3},{8,10},{9,11},{16,18},{17,19},{24,26},{25,27},{32,34},... | collective-permute-start | bytes 4718600 | tf_op jit(solution)/shard_map/ppermute | solution.py:106
  249.6 62.1 %copy-start.2 = (bf16[16,128,384]{2,1,0:T(8,128)(2,1)}, bf16[16,128,384]{2,1,0:T(8,128)(2,1)S(1)}, u32[]{:S(2)}) copy-start(bf16[16,128,384]{2,1,0:T(8,128)(2,1)S(1)} %collective-permute-done) | copy-start | bytes 4718596
  344.5 3.5 collective-permute-start.3
Sparse Core Ops, SparseCore 0:
  54.9 109.6 all-gather.1
  177.6 130.1 reduce-scatter.1

commit v10 on v9

--- a/solution.py
+++ b/solution.py
@@ -20,7 +20,7 @@
 GROUP = 16
 
 
-def _slot_products(pairs, gathered, docs, prefix, live=None, factor=None):
+def _slot_products(pairs, gathered, docs, prefix, live=None, factor=None, group=GROUP):
     slots = pairs.shape[0]
     _, per_shard, rows, width = gathered.shape
     n_docs = docs.shape[-3]
@@ -32,15 +32,15 @@
             return pl.BlockSpec(
                 (1, 1, band, width),
                 lambda i, ids, *_: (
-                    ids[i * GROUP + g] // n_docs // local,
+                    ids[i * group + g] // n_docs // local,
                     local,
-                    half * local + ids[i * GROUP + g] // n_docs % local,
+                    half * local + ids[i * group + g] // n_docs % local,
                     0,
                 ),
             )
         return pl.BlockSpec(
             (1, 1, rows, width),
-            lambda i, ids, *_: (ids[i * GROUP + g] // n_docs // local, ids[i * GROUP + g] // n_docs % local, 0, 0),
+            lambda i, ids, *_: (ids[i * group + g] // n_docs // local, ids[i * group + g] // n_docs % local, 0, 0),
         )
 
     halves = 2 if prefix else 1
@@ -51,10 +51,10 @@
     def kernel(ids, *refs):
         live_ref = refs[0] if live is not None else None
         refs = refs[scalars - 1 :]
-        picked, doc_ref, out = refs[: GROUP * halves], refs[GROUP * halves], refs[-1]
+        picked, doc_ref, out = refs[: group * halves], refs[group * halves], refs[-1]
         step = pl.program_id(0)
-        for g in range(GROUP):
-            d = ids[step * GROUP + g] % n_docs
+        for g in range(group):
+            d = ids[step * group + g] % n_docs
             if prefix:
                 term = lax.dot_general(
                     picked[2 * g][0, 0], doc_ref[0, d], dims, preferred_element_type=jnp.float32
@@ -66,17 +66,17 @@
                     picked[g][0, 0], doc_ref[d], dims, preferred_element_type=jnp.float32
                 )
             if live is not None:
-                slot = step * GROUP + g
+                slot = step * group + g
                 term = jnp.where(slot < live_ref[0], term * factor, jnp.zeros_like(term))
             out[g] = term
 
-    in_specs = [spec(g, h) for g in range(GROUP) for h in range(halves)]
+    in_specs = [spec(g, h) for g in range(group) for h in range(halves)]
     in_specs.append(pl.BlockSpec(docs.shape, lambda i, ids, *_: (0,) * docs.ndim))
     grid_spec = pltpu.PrefetchScalarGridSpec(
         num_scalar_prefetch=scalars,
-        grid=(slots // GROUP,),
+        grid=(slots // group,),
         in_specs=in_specs,
-        out_specs=pl.BlockSpec((GROUP, band, DB), lambda i, ids, *_: (i, 0, 0)),
+        out_specs=pl.BlockSpec((group, band, DB), lambda i, ids, *_: (i, 0, 0)),
     )
     cost = pl.CostEstimate(
         flops=2 * slots * band * DB * width * halves,
@@ -89,7 +89,7 @@
         grid_spec=grid_spec,
         compiler_params=pltpu.CompilerParams(dimension_semantics=("arbitrary",)),
         cost_estimate=cost,
-    )(pairs, *(() if live is None else (live,)), *([gathered] * (GROUP * halves)), docs)
+    )(pairs, *(() if live is None else (live,)), *([gathered] * (group * halves)), docs)
 
 
 def _shards(queries, doc_vectors, surv_pairs, surv_count, short_pairs, short_count):
@@ -123,7 +123,7 @@
     )
 
     full_terms = _slot_products(
-        short_pairs[0], gathered, doc_blocks, False, short_count, float(D) ** (-0.5)
+        short_pairs[0], gathered, doc_blocks, False, short_count, float(D) ** (-0.5), 2 * GROUP
     )
     full_out = lax.psum_scatter(full_terms, DIMS, scatter_dimension=1, tiled=True)
     prefix_sum = _slot_products(surv_pairs[0], gathered, prefix_docs, True)

time: 390 us -> 390 us (level)
  no operation moved by 1% of the time
where the time goes in v10:
time: 390 us; the launch traced here: 388 us
  waiting for transfers between devices  267 us (68%)
  blocking collectives  46.3 us (12%)
  Pallas kernels  41.3 us (11%)
  between operations  15.4 us (4%)
  starting transfers between devices  10.7 us (3%)
  other arithmetic  4.82 us (1%)
    ppermute x3, waiting for transfers between devices, _shards(): lax.ppermute(doc_blocks, DIMS, perm=[(c, far * n_c + c) for c in range(n_...  155 us
    all_gather x1, waiting for transfers between devices, _shards(): gathered = lax.all_gather(near, ('y', 'x'), axis=0, tiled=True)  109 us
    pallas_call x2, Pallas kernels, _slot_products(): pl.pallas_call(kernel, out_shape=jax.ShapeDtypeStruct((slots, band, DB),...  41.3 us
    all_gather x1, blocking collectives, _shards(): near = lax.all_gather(payload, 'zh', axis=0, tiled=True)  28.1 us
    all_to_all x1, blocking collectives, _shards(): spread = lax.all_to_all(by_band, DIMS, 0, 0, tiled=True)  18.2 us
    ppermute x3, starting transfers between devices, _shards(): lax.ppermute(doc_blocks, DIMS, perm=[(c, far * n_c + c) for c in range(n_...  10.5 us
  transfers between devices with their start and end apart: 6, of which 5 were waited for; matrix products, arithmetic and copies ran while one was open for 1% of the time, Pallas kernels for 7%

profile of v10, /device:TPU:2, one launch (start us, length us, event | category | flops | bytes accessed | tf_op | source)
XLA Modules:
  0.0 387.7 jit_solution(8954410292743009169)
XLA Ops:
  7.2 0.0 copy-start.1
  7.2 0.0 all-gather.2.cloned.1.call-start
  7.2 1.1 copy.10
  8.3 18.2 %all_to_all.5 = bf16[8,4,16,384]{3,2,1,0:T(8,128)(2,1)S(1)} all-to-all(bf16[8,4,16,384]{3,2,1,0:T(8,128)(2,1)S(1)} %bitcast.86), channel_id=1, replica_groups=mesh['y'=4,'x'=4,'zh'=2,'zl'=4,'c'=2] {'zl','c'}, dimensions={0} | all-to-all | bytes 786432 | tf_op jit(solution)/shard_map/all_to_all | solution.py:110
  26.5 0.0 copy-done.1
  26.5 0.1 pad_maximum_fusion
  26.6 28.1 %all_gather.6 = bf16[1280,384]{1,0:T(8,128)(2,1)} all-gather(bf16[640,384]{1,0:T(8,128)(2,1)S(1)} %pad_maximum_fusion), channel_id=1, replica_groups=mesh['y'=4,'x'=4,'zh'=2,'zl'=4,'c'=2] {'zh'}, dimensions={0}, use_global_device_ids=true | all-gather | bytes 1474560 | tf_op jit(solution)/shard_map/all_gather | solution.py:113
  54.7 0.0 all-gather.2.cloned.1.call-update
  54.7 0.0 reduce-scatter.2.cloned.1.call-start
  55.4 109.1 %all-gather.2.cloned.1.call-done = bf16[20480,384]{1,0:T(8,128)(2,1)} async-done(((bf16[1280,384]{1,0:T(8,128)(2,1)}), bf16[20480,384]{1,0:T(8,128)(2,1)}) %all-gather.2.cloned.1.call-update) | async-done | bytes 15728656 | tf_op jit(solution)/shard_map/all_gather | solution.py:114
  164.5 12.9 %shard_map.78 = f32[96,128,128]{2,1,0:T(8,128)} custom-call(s32[96]{0:T(128)} %bitcast.91, s32[1]{0:T(128)S(6)} %copy.12.refs_0_, bf16[32,5,128,384]{3,2,1,0:T(8,128)(2,1)} %bitcast.47, bf16[32,5,128,384]{3,2,1,0:T(8,128)(2,1)} %bitcast.17, bf16[32,5,128,384]{3,2,1,0:T(8,128)(2,1)} %bitcast.18, bf16[32,5,128,384]{3,2,1,0:T(8,128)(2,1)} %bitcast.19, ...), custom_call_target="tpu_custom_call" | custom-call | flops 1207959552 | bytes 17301504 | tf_op jit(solution)/shard_map/pallas_call | solution.py:86
  177.5 0.0 copy-start
  177.5 0.0 reduce-scatter.2.cloned.1.call-update
  177.5 1.4 copy-done
  178.9 5.5 %collective-permute-start = (bf16[16,128,384]{2,1,0:T(8,128)(2,1)S(1)}, bf16[16,128,384]{2,1,0:T(8,128)(2,1)S(1)}, u32[]{:S(2)}, u32[]{:S(2)}) collective-permute-start(bf16[16,128,384]{2,1,0:T(8,128)(2,1)S(1)} %bitcast.81), channel_id=1, source_target_pairs={{0,6},{1,7},{8,14},{9,15},{16,22},{17,23},{24,30},{25,31},{32,38},... | collective-permute-start | bytes 4718600 | tf_op jit(solution)/shard_map/ppermute | solution.py:106
  184.4 2.5 collective-permute-start.1
  186.9 2.5 collective-permute-start.2
  189.4 60.3 %collective-permute-done = bf16[16,128,384]{2,1,0:T(8,128)(2,1)S(1)} collective-permute-done((bf16[16,128,384]{2,1,0:T(8,128)(2,1)S(1)}, bf16[16,128,384]{2,1,0:T(8,128)(2,1)S(1)}, u32[]{:S(2)}, u32[]{:S(2)}) %collective-permute-start) | collective-permute-done | bytes 1572896 | tf_op jit(solution)/shard_map/ppermute | solution.py:106
  249.6 0.0 copy-start.2
  249.6 62.1 %collective-permute-done.1 = bf16[16,128,384]{2,1,0:T(8,128)(2,1)} collective-permute-done((bf16[16,128,384]{2,1,0:T(8,128)(2,1)S(1)}, bf16[16,128,384]{2,1,0:T(8,128)(2,1)}, u32[]{:S(2)}, u32[]{:S(2)}) %collective-permute-start.1) | collective-permute-done | bytes 1572896 | tf_op jit(solution)/shard_map/ppermute | solution.py:106
  311.8 0.0 copy-done.2
  311.8 32.4 %collective-permute-done.2 = bf16[16,128,384]{2,1,0:T(8,128)(2,1)} collective-permute-done((bf16[16,128,384]{2,1,0:T(8,128)(2,1)S(1)}, bf16[16,128,384]{2,1,0:T(8,128)(2,1)}, u32[]{:S(2)}, u32[]{:S(2)}) %collective-permute-start.2) | collective-permute-done | bytes 1572896 | tf_op jit(solution)/shard_map/ppermute | solution.py:106
  344.2 0.3 select_select_fusion
  344.5 0.1 collective-permute-start.3
  345.3 2.7 collective-permute-done.3
  348.0 1.9 maximum_select_fusion.refs_32_
  350.0 28.4 %shard_map.77 = f32[144,16,128]{2,1,0:T(8,128)} custom-call(s32[144]{0:T(256)} %bitcast.90, bf16[32,5,128,384]{3,2,1,0:T(8,128)(2,1)} %bitcast.48, bf16[32,5,128,384]{3,2,1,0:T(8,128)(2,1)} %bitcast.49, bf16[32,5,128,384]{3,2,1,0:T(8,128)(2,1)} %bitcast.50, bf16[32,5,128,384]{3,2,1,0:T(8,128)(2,1)} %bitcast.51, bf16[32,5,128,384]{3,2,1,0:T(8,128)(2,1)} %bitcast.52, ...), custom_call_target="tpu_custom_call" | custom-call | flops 452984832 | bytes 7864320 | tf_op jit(solution)/shard_map/pallas_call | solution.py:86
  378.3 2.5 select_bitcast_fusion
  380.8 0.0 reduce-scatter.2.cloned.1.call-done
  (2 shorter events, 0.0 us)
Async XLA Ops:
  7.2 19.4 %copy-start.1 = (bf16[512,384]{1,0:T(8,128)(2,1)S(1)}, bf16[512,384]{1,0:T(8,128)(2,1)}, u32[]{:S(2)}) copy-start(bf16[512,384]{1,0:T(8,128)(2,1)} %param.6) | copy-start | bytes 1179652
  7.2 157.4 %all-gather.2.cloned.1.call-start = ((), (), s32[]{:S(2)}) async-start(), calls=%async_computation.2 | async-start | bytes 16711680 | tf_op jit(solution)/shard_map/all_gather | solution.py:114
  54.7 326.1 %reduce-scatter.2.cloned.1.call-start = ((), (), s32[]{:S(2)}) async-start(), calls=%async_computation.3 | async-start | bytes 7077888 | tf_op jit(solution)/shard_map/reduce_scatter | solution.py:128
  177.5 1.4 copy-start
  178.9 70.7 %collective-permute-start = (bf16[16,128,384]{2,1,0:T(8,128)(2,1)S(1)}, bf16[16,128,384]{2,1,0:T(8,128)(2,1)S(1)}, u32[]{:S(2)}, u32[]{:S(2)}) collective-permute-start(bf16[16,128,384]{2,1,0:T(8,128)(2,1)S(1)} %bitcast.81), channel_id=1, source_target_pairs={{0,6},{1,7},{8,14},{9,15},{16,22},{17,23},{24,30},{25,31},{32,38},... | collective-permute-start | bytes 4718600 | tf_op jit(solution)/shard_map/ppermute | solution.py:106
  184.4 127.4 %collective-permute-start.1 = (bf16[16,128,384]{2,1,0:T(8,128)(2,1)S(1)}, bf16[16,128,384]{2,1,0:T(8,128)(2,1)}, u32[]{:S(2)}, u32[]{:S(2)}) collective-permute-start(bf16[16,128,384]{2,1,0:T(8,128)(2,1)S(1)} %bitcast.82), channel_id=1, source_target_pairs={{0,4},{1,5},{8,12},{9,13},{16,20},{17,21},{24,28},{25,29},{32,36},... | collective-permute-start | bytes 4718600 | tf_op jit(solution)/shard_map/ppermute | solution.py:106
  186.9 157.3 %collective-permute-start.2 = (bf16[16,128,384]{2,1,0:T(8,128)(2,1)S(1)}, bf16[16,128,384]{2,1,0:T(8,128)(2,1)}, u32[]{:S(2)}, u32[]{:S(2)}) collective-permute-start(bf16[16,128,384]{2,1,0:T(8,128)(2,1)S(1)} %bitcast.83), channel_id=1, source_target_pairs={{0,2},{1,3},{8,10},{9,11},{16,18},{17,19},{24,26},{25,27},{32,34},... | collective-permute-start | bytes 4718600 | tf_op jit(solution)/shard_map/ppermute | solution.py:106
  249.6 62.1 %copy-start.2 = (bf16[16,128,384]{2,1,0:T(8,128)(2,1)}, bf16[16,128,384]{2,1,0:T(8,128)(2,1)S(1)}, u32[]{:S(2)}) copy-start(bf16[16,128,384]{2,1,0:T(8,128)(2,1)S(1)} %collective-permute-done) | copy-start | bytes 4718596
  344.5 3.5 collective-permute-start.3
Sparse Core Ops, SparseCore 0:
  54.9 109.6 all-gather.1
  177.6 130.1 reduce-scatter.1
